TPU v7x, 256 devices: a whole 4x4x8 slice. The times are simulated.
256 devices in a mesh: gx: 16 (over x, y), gy: 16 (over z, core).
Axes of the slice: x: 4, y: 4, z: 8, core: 2. Of those that a mesh axis runs over, the one named last changes fastest.
Arguments:
- inv_factors: float32 [64, 64, 4096], P('gx', 'gy'), as said below
- couplings: float32 [64, 64, 2, 4096], P('gx', 'gy'), may hold values from -1.5 to 1.5
- stencil: int32 [64, 64, 2], P('gx', 'gy'), may hold values from 0 to 1
- coarse: int32 [64, 64], P('gx', 'gy'), may hold values from 0 to 1, as said below
Outputs:
- strength: float32 [64, 64, 2], P('gx', 'gy')
- restriction: bfloat16 [3072, 14, 4096], P(('gx', 'gy'))
Inputs may be any that keep to these rules, and one draw needn't show every extreme that they name: Each block of inv_factors is lower triangular with diagonal entries between 0.5 and 1. Each tile of 4 x 4 elements has at most 12 coarse elements, and some tile has exactly 12.
All inputs are finite; a program needn't handle non-finite values.
Results may differ from a plain program's by a relative error of at most 0.001.
Values sent between devices are 32-bit elements; how exact they have to be, the bound alone decides.
No kernel may reach another device: no remote copies, remote signals or barrier semaphores. Data moves between devices by JAX's collectives and lax.ppermute only.
A program may use at most 64 MiB of HBM per device.

v0:
```python
import math

import jax
import jax.numpy as jnp
from jax import lax
from jax.sharding import PartitionSpec as P

CAP = 12
PREC = lax.Precision.HIGH


def matmul(left_block, right_block):
    return jnp.einsum("...ij,...jk->...ik", left_block, right_block, precision=PREC)


def left_gram(left_block, right_block):
    return jnp.einsum("...ji,...jk->...ik", left_block, right_block, precision=PREC)


def right_gram(left_block, right_block):
    return jnp.einsum("...ij,...kj->...ik", left_block, right_block, precision=PREC)


def crop_cycle(values, margin):
    return values[margin : values.shape[0] - margin, margin : values.shape[1] - margin]


def upwind_pick(values, upwind_side):
    trailing = (1,) * (values.ndim - 2)
    sign_x = upwind_side[:, :, 0].reshape(upwind_side.shape[:2] + trailing)
    sign_y = upwind_side[:, :, 1].reshape(upwind_side.shape[:2] + trailing)
    upwind_x = jnp.where(sign_x == 1, values[2:, 1:-1], values[:-2, 1:-1])
    upwind_y = jnp.where(sign_y == 1, values[1:-1, 2:], values[1:-1, :-2])
    return (upwind_x, upwind_y)


def shift_pairs(count, step):
    return [(i, i + step) for i in range(count) if 0 <= i + step < count]


def corner_pairs(n_x, n_y, step_x, step_y):
    pairs = []
    for a in range(n_x):
        for b in range(n_y):
            if 0 <= a + step_x < n_x and 0 <= b + step_y < n_y:
                pairs.append((a * n_y + b, (a + step_x) * n_y + (b + step_y)))
    return pairs


def code_block(codes, order):
    values = codes.reshape(1, -1).astype(jnp.float32)
    return jnp.pad(values, ((0, order - 1), (0, order - values.shape[1])))[None]


def row_band(pieces):
    return jnp.concatenate(pieces, axis=1)


def padded(values, before_x, before_y):
    widths = [(1, 0) if before_x else (0, 1), (1, 0) if before_y else (0, 1)]
    widths += [(0, 0)] * (values.ndim - 2)
    return jnp.pad(values, widths)


def on_device(inv_factors, couplings, stencil, coarse):
    nx, ny, flat = inv_factors.shape
    order = math.isqrt(flat)
    blk = (order, order)
    n_gx = lax.axis_size("gx")
    n_gy = lax.axis_size("gy")
    total_x = nx * n_gx
    total_y = ny * n_gy
    coord_x = lax.axis_index("gx") * nx + jnp.arange(nx, dtype=jnp.int32)
    coord_y = lax.axis_index("gy") * ny + jnp.arange(ny, dtype=jnp.int32)
    target_x = coord_x[:, None] + 2 * stencil[:, :, 0] - 1
    target_y = coord_y[None, :] + 2 * stencil[:, :, 1] - 1
    reach = jnp.stack(
        [(target_x >= 0) & (target_x < total_x), (target_y >= 0) & (target_y < total_y)], axis=-1
    )
    minus_own = (couplings * (-reach.astype(jnp.float32))[:, :, :, None]).reshape(
        (nx, ny, 2) + blk
    )
    factor_own = inv_factors.reshape((nx, ny) + blk)
    fine_own = (1 - coarse).astype(jnp.float32)[:, :, None, None] * left_gram(
        factor_own, factor_own
    )
    lead_own = matmul(fine_own[:, :, None], minus_own)

    def face(rows, cols):
        return jnp.concatenate(
            [
                fine_own[rows[3], cols[3]].reshape((-1,) + blk),
                lead_own[rows[2], cols[2]].reshape((-1,) + blk),
                factor_own[rows[1], cols[1]].reshape((-1,) + blk),
                code_block(stencil[rows[2], cols[2]], order),
            ],
            axis=0,
        )

    every = {d: slice(None) for d in (1, 2, 3)}
    low = {d: slice(0, d) for d in (1, 2, 3)}
    high_x = {d: slice(nx - d, nx) for d in (1, 2, 3)}
    high_y = {d: slice(ny - d, ny) for d in (1, 2, 3)}
    from_xlo = lax.ppermute(face(high_x, every), "gx", shift_pairs(n_gx, 1))
    from_xhi = lax.ppermute(face(low, every), "gx", shift_pairs(n_gx, -1))
    from_ylo = lax.ppermute(face(every, high_y), "gy", shift_pairs(n_gy, 1))
    from_yhi = lax.ppermute(face(every, low), "gy", shift_pairs(n_gy, -1))

    corners = {}
    for sx in (1, -1):
        for sy in (1, -1):
            rows2 = slice(nx - 2, nx) if sx == 1 else slice(0, 2)
            cols2 = slice(ny - 2, ny) if sy == 1 else slice(0, 2)
            row1 = nx - 1 if sx == 1 else 0
            col1 = ny - 1 if sy == 1 else 0
            buffer = jnp.concatenate(
                [
                    fine_own[rows2, cols2].reshape((-1,) + blk),
                    lead_own[row1, col1],
                    code_block(stencil[row1, col1], order),
                ],
                axis=0,
            )
            corners[(sx, sy)] = lax.ppermute(
                buffer, ("gx", "gy"), corner_pairs(n_gx, n_gy, sx, sy)
            )

    def unpack_face(buffer, count, along_x):
        n_p, n_w = 3 * count, 2 * count * 2
        p_part = buffer[0:n_p]
        w_part = buffer[n_p : n_p + n_w]
        g_part = buffer[n_p + n_w : n_p + n_w + count]
        codes = buffer[n_p + n_w + count, 0, 0 : 2 * count * 2].astype(jnp.int32)
        if along_x:
            return (p_part.reshape((3, count) + blk), w_part.reshape((2, count, 2) + blk),
                    g_part.reshape((1, count) + blk), codes.reshape(2, count, 2))
        return (p_part.reshape((count, 3) + blk), w_part.reshape((count, 2, 2) + blk),
                g_part.reshape((count, 1) + blk), codes.reshape(count, 2, 2))

    pxl, wxl, gxl, cxl = unpack_face(from_xlo, ny, True)
    pxh, wxh, gxh, cxh = unpack_face(from_xhi, ny, True)
    pyl, wyl, gyl, cyl = unpack_face(from_ylo, nx, False)
    pyh, wyh, gyh, cyh = unpack_face(from_yhi, nx, False)

    def unpack_corner(buffer):
        return (buffer[0:4].reshape((2, 2) + blk), buffer[4:6].reshape((1, 1, 2) + blk),
                buffer[6, 0, 0:2].astype(jnp.int32).reshape(1, 1, 2))

    c_ll = unpack_corner(corners[(1, 1)])
    c_lh = unpack_corner(corners[(1, -1)])
    c_hl = unpack_corner(corners[(-1, 1)])
    c_hh = unpack_corner(corners[(-1, -1)])

    def cycle(k, lo_x, own, hi_x, lo_y, hi_y):
        return jnp.concatenate(
            [
                row_band([padded(c_ll[k], True, True), lo_x, padded(c_lh[k], True, False)]),
                row_band([lo_y, own, hi_y]),
                row_band([padded(c_hl[k], False, True), hi_x, padded(c_hh[k], False, False)]),
            ],
            axis=0,
        )

    fine_cycle = cycle(0, pxl, fine_own, pxh, pyl, pyh)
    lead_cycle = cycle(1, wxl, lead_own, wxh, wyl, wyh)
    side_cycle = cycle(2, cxl, stencil, cxh, cyl, cyh)
    corner_zero = jnp.zeros((1, 1) + blk, jnp.float32)
    factor_cycle = jnp.concatenate(
        [
            row_band([corner_zero, gxl, corner_zero]),
            row_band([gyl, factor_own, gyh]),
            row_band([corner_zero, gxh, corner_zero]),
        ],
        axis=0,
    )

    up_x, up_y = upwind_pick(fine_cycle, side_cycle)
    near = jnp.stack(
        [crop_cycle(fine_cycle, 1), matmul(lead_cycle[:, :, 0], up_x),
         matmul(lead_cycle[:, :, 1], up_y)],
        axis=2,
    )
    near_x, near_y = upwind_pick(near, crop_cycle(side_cycle, 1))
    lead_6 = crop_cycle(lead_cycle, 1)
    far = jnp.concatenate(
        [
            crop_cycle(fine_cycle, 2)[:, :, None],
            matmul(lead_6[:, :, 0:1], near_x),
            matmul(lead_6[:, :, 1:2], near_y),
        ],
        axis=2,
    )

    gup_x, gup_y = upwind_pick(factor_cycle, stencil)
    scaled_left = matmul(factor_own[:, :, None], minus_own)
    strong = []
    for direction, gup in ((0, gup_x), (1, gup_y)):
        scaled = right_gram(scaled_left[:, :, direction], gup)
        strong.append(jnp.mean(scaled * scaled, axis=(-2, -1)))
    strong = jnp.stack(strong, axis=-1)

    cell_count = nx * ny
    flat_coarse = coarse.reshape(cell_count)
    slot_rank = jnp.cumsum(flat_coarse, dtype=jnp.int32) - flat_coarse
    chosen = (
        (slot_rank[None, :] == jnp.arange(CAP, dtype=jnp.int32)[:, None])
        & (flat_coarse[None, :] == 1)
    ).astype(jnp.int32)
    source = jnp.sum(
        chosen * jnp.arange(cell_count, dtype=jnp.int32)[None, :], axis=1, dtype=jnp.int32
    )
    filled = jnp.sum(chosen, axis=1, dtype=jnp.int32)
    span = ny + 2
    own_i = jnp.arange(nx, dtype=jnp.int32)[:, None] + 1
    own_j = jnp.arange(ny, dtype=jnp.int32)[None, :] + 1
    up_index = jnp.stack(
        [(own_i + 2 * stencil[:, :, 0] - 1) * span + own_j,
         own_i * span + own_j + 2 * stencil[:, :, 1] - 1],
        axis=-1,
    ).reshape(cell_count, 2)
    picked = jnp.take(up_index, source, axis=0, mode="clip").reshape(CAP * 2)
    far_rows = jnp.take(far.reshape(((nx + 2) * (ny + 2), 7) + blk), picked, axis=0,
                        mode="clip").reshape((CAP, 2, 7) + blk)
    coupling_rows = jnp.take(minus_own.reshape((cell_count, 2) + blk), source, axis=0,
                             mode="clip")
    restrict = matmul(coupling_rows[:, :, None], far_rows)
    restrict = (restrict * filled[:, None, None, None, None].astype(restrict.dtype)).astype(
        jnp.bfloat16
    )
    return (strong, restrict.reshape(CAP, 14, flat))


def solution(mesh):
    placed = (P("gx", "gy", None), P("gx", "gy", None, None), P("gx", "gy", None), P("gx", "gy"))
    return jax.shard_map(
        on_device,
        mesh=mesh,
        in_specs=placed,
        out_specs=(P("gx", "gy", None), P(("gx", "gy"), None, None)),
        check_vma=False,
    )
```

profile of v0, /device:TPU:120, one launch (start us, length us, event | category | flops | bytes accessed | tf_op | source)
XLA Modules:
  0.0 193.1 jit_solution(15343483376266436999)
XLA Ops:
  2.2 1.4 broadcast_compare_fusion.1
  4.3 1.2 squeeze_broadcast_in_dim_reshape.3
  10.5 1.5 pad_maximum_fusion.24
  12.0 2.0 %collective-permute-start.5 = (f32[7,64,64]{1,2,0:T(8,128)}, f32[7,64,64]{1,2,0:T(8,128)}, u32[]{:S(2)}, u32[]{:S(2)}) collective-permute-start(f32[7,64,64]{1,2,0:T(8,128)} %pad_maximum_fusion.24), channel_id=1, source_target_pairs={{1,16},{2,17},{3,18},{4,19},{5,20},{6,21},{7,22},{8,23},{9,24},{10... | collective-permute-start | bytes 344072 | tf_op jit(solution)/shard_map/ppermute | solution.py:124
  14.6 1.0 copy.258
  15.6 1.6 pad_maximum_fusion.25
  17.2 3.5 %collective-permute-start.6 = (f32[7,64,64]{1,2,0:T(8,128)}, f32[7,64,64]{1,2,0:T(8,128)}, u32[]{:S(2)}, u32[]{:S(2)}) collective-permute-start(f32[7,64,64]{1,2,0:T(8,128)} %pad_maximum_fusion.25), channel_id=1, source_target_pairs={{16,1},{17,2},{18,3},{19,4},{20,5},{21,6},{22,7},{23,8},{24,9},{25... | collective-permute-start | bytes 344072 | tf_op jit(solution)/shard_map/ppermute | solution.py:124
  21.4 1.6 pad_maximum_fusion.26
  23.0 2.5 %collective-permute-start.7 = (f32[7,64,64]{1,2,0:T(8,128)}, f32[7,64,64]{1,2,0:T(8,128)}, u32[]{:S(2)}, u32[]{:S(2)}) collective-permute-start(f32[7,64,64]{1,2,0:T(8,128)} %pad_maximum_fusion.26), channel_id=1, source_target_pairs={{17,0},{18,1},{19,2},{20,3},{21,4},{22,5},{23,6},{24,7},{25,8},{26... | collective-permute-start | bytes 344072 | tf_op jit(solution)/shard_map/ppermute | solution.py:124
  25.7 1.6 pad_maximum_fusion.23
  27.2 6.1 %collective-permute-start.4 = (f32[7,64,64]{1,2,0:T(8,128)}, f32[7,64,64]{1,2,0:T(8,128)}, u32[]{:S(2)}, u32[]{:S(2)}) collective-permute-start(f32[7,64,64]{1,2,0:T(8,128)} %pad_maximum_fusion.23), channel_id=1, source_target_pairs={{0,17},{1,18},{2,19},{3,20},{4,21},{5,22},{6,23},{7,24},{8,25},{9,... | collective-permute-start | bytes 344072 | tf_op jit(solution)/shard_map/ppermute | solution.py:124
  38.6 1.0 copy.236
  39.6 2.3 %pad_maximum_fusion.2 = f32[33,64,64]{2,1,0:T(8,128)} fusion(f32[1,64,64]{2,1,0:T(8,128)} %pad_bitcast_fusion.7, f32[4,64,64]{2,1,0:T(8,128)S(1)} %get-tuple-element.35, f32[16,64,64]{2,1,0:T(8,128)} %copy.236, f32[12,64,64]{2,1,0:T(8,128)} %bitcast.193), kind=kLoop, calls=%fused_computation.61 | loop fusion | flops 405504 | bytes 1081344 | tf_op jit(solution)/shard_map/concatenate | solution.py:90
  41.9 5.0 %collective-permute-start = (f32[33,64,64]{2,1,0:T(8,128)}, f32[33,64,64]{2,1,0:T(8,128)}, u32[]{:S(2)}, u32[]{:S(2)}) collective-permute-start(f32[33,64,64]{2,1,0:T(8,128)} %pad_maximum_fusion.2), channel_id=1, source_target_pairs={{0,1},{1,2},{2,3},{3,4},{4,5},{5,6},{6,7},{7,8},{8,9},{9,10},{10,1... | collective-permute-start | bytes 1622024 | tf_op jit(solution)/shard_map/ppermute | solution.py:106
  50.6 1.1 fusion.57
  52.9 1.3 stack.37
  59.7 1.3 select_reduce_fusion
  62.6 1.2 pad_bitcast_fusion.4
  63.8 1.3 pad_bitcast_fusion.5
  65.1 1.6 reshape.496
  66.7 1.6 reshape.500
  68.3 2.1 %convolution_bitcast_fusion.1 = f32[4,4,2,64,64]{3,4,2,1,0:T(8,128)} fusion(f32[4,4,2,64,64]{4,3,2,1,0:T(8,128)S(1)} %reshape.485, f32[4,4,64,64,1]{3,2,1,0,4:T(8,128)S(1)} %reshape.554), kind=kOutput, calls=%fused_computation.53 | convolution fusion | flops 50331648 | bytes 1310720 | tf_op jit(solution)/shard_map/...ij,...jk->...ik/dot_general | solution.py:13
  71.4 2.0 %pad_maximum_fusion.4 = f32[33,64,64]{2,1,0:T(8,128)} fusion(f32[1,64,64]{2,1,0:T(8,128)} %pad_bitcast_fusion.5, f32[4,64,64]{2,1,0:T(8,128)} %reshape.496, f32[16,64,64]{2,1,0:T(8,128)S(1)} %copy.244, f32[12,64,64]{2,1,0:T(8,128)S(1)} %bitcast.192), kind=kLoop, calls=%fused_computation.63 | loop fusion | flops 405504 | bytes 1081344 | tf_op jit(solution)/shard_map/concatenate | solution.py:90
  73.4 1.8 pad_maximum_fusion.5
  75.2 1.1 pad_maximum_fusion.3
  79.3 1.5 gather_fusion.2
  80.8 1.9 collective-permute-start.1
  82.7 1.5 slice_bitcast_fusion.25
  84.2 3.0 %collective-permute-start.3 = (f32[33,64,64]{2,1,0:T(8,128)S(1)}, f32[33,64,64]{2,1,0:T(8,128)}, u32[]{:S(2)}, u32[]{:S(2)}) collective-permute-start(f32[33,64,64]{2,1,0:T(8,128)S(1)} %copy-done.14), channel_id=1, source_target_pairs={{0,16},{16,32},{32,48},{48,64},{64,80},{80,96},{96,112},{112,128},... | collective-permute-start | bytes 1622024 | tf_op jit(solution)/shard_map/ppermute | solution.py:104
  87.3 1.5 slice_bitcast_fusion.24
  88.7 3.0 %collective-permute-start.2 = (f32[33,64,64]{2,1,0:T(8,128)}, f32[33,64,64]{2,1,0:T(8,128)S(1)}, u32[]{:S(2)}, u32[]{:S(2)}) collective-permute-start(f32[33,64,64]{2,1,0:T(8,128)} %pad_maximum_fusion.4), channel_id=1, source_target_pairs={{16,0},{32,16},{48,32},{64,48},{80,64},{96,80},{112,96},{128,112},... | collective-permute-start | bytes 1622024 | tf_op jit(solution)/shard_map/ppermute | solution.py:105
  91.7 1.5 slice_bitcast_fusion.23
  93.8 1.5 slice_bitcast_fusion.26
  104.9 7.6 %collective-permute-done.3 = f32[33,64,64]{2,1,0:T(8,128)} collective-permute-done((f32[33,64,64]{2,1,0:T(8,128)S(1)}, f32[33,64,64]{2,1,0:T(8,128)}, u32[]{:S(2)}, u32[]{:S(2)}) %collective-permute-start.3) | collective-permute-done | bytes 540704 | tf_op jit(solution)/shard_map/ppermute | solution.py:104
  113.3 5.6 %collective-permute-done.2 = f32[33,64,64]{2,1,0:T(8,128)S(1)} collective-permute-done((f32[33,64,64]{2,1,0:T(8,128)}, f32[33,64,64]{2,1,0:T(8,128)S(1)}, u32[]{:S(2)}, u32[]{:S(2)}) %collective-permute-start.2) | collective-permute-done | bytes 540704 | tf_op jit(solution)/shard_map/ppermute | solution.py:105
  119.8 1.0 slice.373
  120.9 1.0 slice.374
  121.9 1.0 slice.369
  123.0 1.4 fusion.10
  124.4 1.1 slice.382
  125.5 1.5 slice_bitcast_fusion.4
  126.9 1.9 slice.396
  128.8 2.0 %copy.273 = f32[16,64,64]{1,2,0:T(8,128)} copy(f32[16,64,64]{2,1,0:T(8,128)} %slice.396) | data formatting | bytes 524288 | tf_op jit(solution)/shard_map/slice | solution.py:131
  132.8 2.1 %fusion.24 = f32[4,4]{1,0:T(4,128)S(1)} fusion(f32[4,4,64,64]{3,2,1,0:T(8,128)} %copy-done.3, f32[4,1,64,64]{3,2,1,0:T(8,128)S(1)} %slice_bitcast_fusion.21, f32[4,1,64,64]{3,2,1,0:T(8,128)S(1)} %slice_bitcast_fusion.19, f32[4,4,2,64,64]{3,4,2,1,0:T(8,128)} %convolution_bitcast_fusion.1, pred[4,4]{1,0:T(4,128)(4,1)S(1)} %bitcast.203), kind=kOutput, calls=%fused_computation.60 | convolution fusion | flops 25493488 | bytes 1179728 | tf_op jit(solution)/shard_map/...ij,...kj->...ik/dot_general | solution.py:21
  134.8 1.9 slice.397
  136.7 2.0 %copy.274 = f32[16,64,64]{1,2,0:T(8,128)} copy(f32[16,64,64]{2,1,0:T(8,128)} %slice.397) | data formatting | bytes 524288 | tf_op jit(solution)/shard_map/slice | solution.py:131
  138.8 1.9 slice.394
  140.7 2.1 %copy.272 = f32[16,64,64]{1,2,0:T(8,128)} copy(f32[16,64,64]{2,1,0:T(8,128)} %slice.394) | data formatting | bytes 524288 | tf_op jit(solution)/shard_map/slice | solution.py:131
  144.6 2.1 %fusion.23 = f32[4,4]{1,0:T(4,128)S(1)} fusion(f32[4,1,64,64]{3,2,1,0:T(8,128)} %copy-done.28, f32[1,1,64,64]{3,2,1,0:T(8,128)S(1)} %broadcast_in_dim.90, f32[4,4,64,64]{3,2,1,0:T(8,128)} %copy-done.3, f32[4,1,64,64]{3,2,1,0:T(8,128)} %copy-done.27, f32[1,4,64,64]{3,2,1,0:T(8,128)S(1)} %slice_bitcast_fusion.17, ...), kind=kOutput, calls=%fused_computation.59 | convolution fusion | flops 26017776 | bytes 1458752 | tf_op jit(solution)/shard_map/...ij,...kj->...ik/dot_general | solution.py:21
  147.3 1.9 slice.399
  149.2 2.0 %copy.275 = f32[16,64,64]{1,2,0:T(8,128)} copy(f32[16,64,64]{2,1,0:T(8,128)} %slice.399) | data formatting | bytes 524288 | tf_op jit(solution)/shard_map/slice | solution.py:131
  151.3 2.7 %copy.282 = f32[36,1,64,64]{2,3,1,0:T(8,128)} copy(f32[36,1,64,64]{3,2,0,1:T(8,128)} %bitcast.177) | data formatting | bytes 1179648 | tf_op jit(solution)/shard_map/concatenate | solution.py:185
  154.0 2.1 %fusion = f32[8,8,2,64,64]{3,4,2,1,0:T(8,128)S(1)} fusion(f32[1,1,2,64,64]{3,4,2,1,0:T(8,128)S(1)} %copy-done.23, f32[1,1,2,64,64]{3,4,2,1,0:T(8,128)S(1)} %copy-done.22, f32[1,1,2,64,64]{3,4,2,1,0:T(8,128)S(1)} %copy-done.21, f32[1,1,2,64,64]{3,4,2,1,0:T(8,128)S(1)} %copy-done.24, f32[2,4,2,64,64]{3,4,2,1,0:T(8,128)} %bitcast.185, ...), kind=kLoop, calls=%fused_computation.7 | loop fusion | flops 12582912 | bytes 3801088 | tf_op jit(solution)/shard_map/concatenate | solution.py:155
  156.1 2.0 %fusion.22 = f32[8,8,1,64,64]{4,3,1,0,2:T(8,128)S(1)} fusion(f32[10,10,64,64]{3,2,1,0:T(8,128)S(1)} %fusion.10, f32[8,8,2,64,64]{3,4,2,1,0:T(8,128)S(1)} %fusion, pred[8,8]{1,0:T(8,128)(4,1)S(1)} %copy-done.33), kind=kOutput, calls=%fused_computation.51 | convolution fusion | flops 100925440 | bytes 7341056 | tf_op jit(solution)/shard_map/...ij,...jk->...ik/dot_general | solution.py:13
  158.1 2.0 %fusion.21 = f32[8,8,1,64,64]{4,3,1,0,2:T(8,128)S(1)} fusion(f32[10,10,64,64]{3,2,1,0:T(8,128)S(1)} %fusion.10, f32[8,8,2,64,64]{3,4,2,1,0:T(8,128)S(1)} %fusion, pred[8,8]{1,0:T(8,128)(4,1)S(1)} %copy-done.32), kind=kOutput, calls=%fused_computation.50 | convolution fusion | flops 100925440 | bytes 7341056 | tf_op jit(solution)/shard_map/...ij,...jk->...ik/dot_general | solution.py:13
  160.1 1.4 pad_maximum_fusion.1
  161.4 2.5 %slice_select_fusion.1 = (f32[6,6,3,64,64]{4,3,1,0,2:T(8,128)S(1)}, f32[6,6,3,64,64]{4,3,1,0,2:T(8,128)S(1)}) fusion(f32[8,8,3,64,64]{4,3,1,0,2:T(8,128)S(1)} %pad_maximum_fusion.1, pred[6,6]{1,0:T(8,128)(4,1)S(1)} %get-tuple-element.38, pred[6,6]{1,0:T(8,128)(4,1)S(1)} %get-tuple-element.39), kind=kLoop, calls=%fused_computation.21 | loop fusion | flops 884736 | bytes 10616904 | tf_op jit(solution)/shard_map/jit(_where)/select_n | solution.py:32
  163.9 3.0 %fusion.8 = f32[6,6,3,64,64]{4,3,2,1,0:T(8,128)S(1)} fusion(f32[6,6,3,64,64]{4,3,1,0,2:T(8,128)S(1)} %get-tuple-element.16, f32[8,8,2,64,64]{3,4,2,1,0:T(8,128)S(1)} %fusion), kind=kOutput, calls=%fused_computation.24 | convolution fusion | flops 169869312 | bytes 6488064 | tf_op jit(solution)/shard_map/...ij,...jk->...ik/dot_general | solution.py:13
  166.9 3.0 %fusion.6 = f32[6,6,3,64,64]{4,3,2,1,0:T(8,128)S(1)} fusion(f32[6,6,3,64,64]{4,3,1,0,2:T(8,128)S(1)} %get-tuple-element.17, f32[8,8,2,64,64]{3,4,2,1,0:T(8,128)S(1)} %fusion), kind=kOutput, calls=%fused_computation.22 | convolution fusion | flops 169869312 | bytes 6488064 | tf_op jit(solution)/shard_map/...ij,...jk->...ik/dot_general | solution.py:13
  169.9 3.7 %pad_maximum_fusion = f32[36,7,64,64]{2,3,1,0:T(8,128)} fusion(f32[36,3,64,64]{2,3,1,0:T(8,128)S(1)} %bitcast.176, f32[36,3,64,64]{2,3,1,0:T(8,128)S(1)} %bitcast.175, f32[36,1,64,64]{2,3,1,0:T(8,128)S(1)} %copy-done.4), kind=kLoop, calls=%fused_computation.3 | loop fusion | flops 2064384 | bytes 8257536 | tf_op jit(solution)/shard_map/concatenate | solution.py:185
  173.6 6.8 %gather_fusion.1 = f32[24,7,64,64]{2,3,1,0:T(8,128)} fusion(f32[36,7,64,64]{2,3,1,0:T(8,128)} %pad_maximum_fusion, s32[1024]{0:T(1024)S(1)} %pad_clamp_fusion), kind=kCustom, calls=%fused_computation.1 | custom fusion | bytes 5505120 | tf_op jit(solution)/shard_map/jit(_take)/gather | solution.py:222
  180.4 5.1 %fusion.16 = bf16[12,2,7,64,64]{3,4,2,1,0:T(8,128)(2,1)S(1)} fusion(f32[12]{0:T(128)S(1)} %copy-done.37, f32[12,2,7,64,64]{3,4,2,1,0:T(8,128)} %bitcast.174, f32[12,2,64,64]{3,2,1,0:T(8,128)S(1)} %copy-done.7), kind=kOutput, calls=%fused_computation.40 | convolution fusion | flops 265617408 | bytes 4522032 | tf_op jit(solution)/shard_map/...ij,...jk->...ik/dot_general | solution.py:13
  185.4 2.7 %copy.285 = bf16[12,2,7,64,64]{4,3,2,1,0:T(8,128)(2,1)} copy(bf16[12,2,7,64,64]{3,4,2,1,0:T(8,128)(2,1)S(1)} %fusion.16) | data formatting | bytes 2752512 | tf_op jit(solution)/shard_map/convert_element_type | solution.py:227
  188.1 5.0 %reshape.526 = bf16[12,14,4096]{2,1,0:T(8,128)(2,1)} reshape(bf16[12,2,7,64,64]{4,3,2,1,0:T(8,128)(2,1)} %copy.285) | data formatting | bytes 2752512 | tf_op jit(solution)/shard_map/reshape | solution.py:230
  (196 shorter events, 46.2 us)
Async XLA Ops:
  0.6 6.4 %copy-start.19 = (f32[4,4,2,4096]{3,2,1,0:T(2,128)S(1)}, f32[4,4,2,4096]{3,2,1,0:T(2,128)}, u32[]{:S(2)}) copy-start(f32[4,4,2,4096]{3,2,1,0:T(2,128)} %param.5) | copy-start | bytes 1572868
  5.6 28.4 %copy-start.3 = (f32[4,4,64,64]{3,2,1,0:T(8,128)}, f32[4,4,64,64]{3,2,1,0:T(8,128)S(1)}, u32[]{:S(2)}) copy-start(f32[4,4,64,64]{3,2,1,0:T(8,128)S(1)} %squeeze_broadcast_in_dim_reshape.3) | copy-start | bytes 786436
  6.2 43.6 %copy-start = (f32[4,4,64,64]{3,2,1,0:T(8,128)}, f32[4,4,64,64]{3,2,1,0:T(8,128)S(1)}, u32[]{:S(2)}) copy-start(f32[4,4,64,64]{3,2,1,0:T(8,128)S(1)} %convolution_multiply_fusion.2) | copy-start | bytes 786436
  7.3 0.8 copy-start.5
  8.8 24.6 %copy-start.25 = (s32[4,4,2]{1,2,0:T(2,128)S(1)}, s32[4,4,2]{1,2,0:T(2,128)}, u32[]{:S(2)}) copy-start(s32[4,4,2]{1,2,0:T(2,128)} %param.6) | copy-start | bytes 388
  9.8 40.8 %copy-start.1 = (f32[4,4,2,64,64]{3,4,2,1,0:T(8,128)}, f32[4,4,2,64,64]{3,4,2,1,0:T(8,128)S(1)}, u32[]{:S(2)}) copy-start(f32[4,4,2,64,64]{3,4,2,1,0:T(8,128)S(1)} %convolution_bitcast_fusion) | copy-start | bytes 1572868
  12.0 68.8 %collective-permute-start.5 = (f32[7,64,64]{1,2,0:T(8,128)}, f32[7,64,64]{1,2,0:T(8,128)}, u32[]{:S(2)}, u32[]{:S(2)}) collective-permute-start(f32[7,64,64]{1,2,0:T(8,128)} %pad_maximum_fusion.24), channel_id=1, source_target_pairs={{1,16},{2,17},{3,18},{4,19},{5,20},{6,21},{7,22},{8,23},{9,24},{10... | collective-permute-start | bytes 344072 | tf_op jit(solution)/shard_map/ppermute | solution.py:124
  17.2 67.0 %collective-permute-start.6 = (f32[7,64,64]{1,2,0:T(8,128)}, f32[7,64,64]{1,2,0:T(8,128)}, u32[]{:S(2)}, u32[]{:S(2)}) collective-permute-start(f32[7,64,64]{1,2,0:T(8,128)} %pad_maximum_fusion.25), channel_id=1, source_target_pairs={{16,1},{17,2},{18,3},{19,4},{20,5},{21,6},{22,7},{23,8},{24,9},{25... | collective-permute-start | bytes 344072 | tf_op jit(solution)/shard_map/ppermute | solution.py:124
  23.0 65.7 %collective-permute-start.7 = (f32[7,64,64]{1,2,0:T(8,128)}, f32[7,64,64]{1,2,0:T(8,128)}, u32[]{:S(2)}, u32[]{:S(2)}) collective-permute-start(f32[7,64,64]{1,2,0:T(8,128)} %pad_maximum_fusion.26), channel_id=1, source_target_pairs={{17,0},{18,1},{19,2},{20,3},{21,4},{22,5},{23,6},{24,7},{25,8},{26... | collective-permute-start | bytes 344072 | tf_op jit(solution)/shard_map/ppermute | solution.py:124
  27.2 66.6 %collective-permute-start.4 = (f32[7,64,64]{1,2,0:T(8,128)}, f32[7,64,64]{1,2,0:T(8,128)}, u32[]{:S(2)}, u32[]{:S(2)}) collective-permute-start(f32[7,64,64]{1,2,0:T(8,128)} %pad_maximum_fusion.23), channel_id=1, source_target_pairs={{0,17},{1,18},{2,19},{3,20},{4,21},{5,22},{6,23},{7,24},{8,25},{9,... | collective-permute-start | bytes 344072 | tf_op jit(solution)/shard_map/ppermute | solution.py:124
  34.6 12.3 %copy-start.29 = (s32[4,4]{1,0:T(4,128)S(1)}, s32[4,4]{1,0:T(4,128)}, u32[]{:S(2)}) copy-start(s32[4,4]{1,0:T(4,128)} %param.7) | copy-start | bytes 196
  34.6 14.2 %copy-start.11 = (f32[4,4,4096]{2,1,0:T(4,128)S(1)}, f32[4,4,4096]{2,1,0:T(4,128)}, u32[]{:S(2)}) copy-start(f32[4,4,4096]{2,1,0:T(4,128)} %param.4) | copy-start | bytes 786436
  41.9 61.2 %collective-permute-start = (f32[33,64,64]{2,1,0:T(8,128)}, f32[33,64,64]{2,1,0:T(8,128)}, u32[]{:S(2)}, u32[]{:S(2)}) collective-permute-start(f32[33,64,64]{2,1,0:T(8,128)} %pad_maximum_fusion.2), channel_id=1, source_target_pairs={{0,1},{1,2},{2,3},{3,4},{4,5},{5,6},{6,7},{7,8},{8,9},{9,10},{10,1... | collective-permute-start | bytes 1622024 | tf_op jit(solution)/shard_map/ppermute | solution.py:106
  48.8 2.9 %copy-start.39 = (s32[16]{0:T(128)S(1)}, s32[16]{0:T(128)}, u32[]{:S(2)}) copy-start(s32[16]{0:T(128)} %reshape.524) | copy-start | bytes 196
  49.7 2.5 %copy-start.34 = (s32[4]{0:T(128)S(1)}, s32[4]{0:T(128)}, u32[]{:S(2)}) copy-start(s32[4]{0:T(128)} %get-tuple-element.56) | copy-start | bytes 52
  49.8 2.5 %copy-start.40 = (s32[4]{0:T(128)S(1)}, s32[4]{0:T(128)}, u32[]{:S(2)}) copy-start(s32[4]{0:T(128)} %get-tuple-element.57) | copy-start | bytes 52
  50.6 20.2 %copy-start.8 = (f32[4,2,2,64,64]{3,4,2,1,0:T(8,128)S(1)}, f32[4,2,2,64,64]{3,4,2,1,0:T(8,128)}, u32[]{:S(2)}) copy-start(f32[4,2,2,64,64]{3,4,2,1,0:T(8,128)} %get-tuple-element.24) | copy-start | bytes 786436
  51.7 18.7 %copy-start.10 = (f32[2,4,2,64,64]{3,4,2,1,0:T(8,128)S(1)}, f32[2,4,2,64,64]{3,4,2,1,0:T(8,128)}, u32[]{:S(2)}) copy-start(f32[2,4,2,64,64]{3,4,2,1,0:T(8,128)} %get-tuple-element.22) | copy-start | bytes 786436
  51.7 18.9 %copy-start.9 = (f32[2,4,2,64,64]{3,4,2,1,0:T(8,128)S(1)}, f32[2,4,2,64,64]{3,4,2,1,0:T(8,128)}, u32[]{:S(2)}) copy-start(f32[2,4,2,64,64]{3,4,2,1,0:T(8,128)} %get-tuple-element.23) | copy-start | bytes 786436
  70.4 1.0 copy-start.13
  70.4 3.0 %copy-start.18 = (f32[4,64,64]{2,1,0:T(8,128)S(1)}, f32[4,64,64]{2,1,0:T(8,128)}, u32[]{:S(2)}) copy-start(f32[4,64,64]{2,1,0:T(8,128)} %reshape.500) | copy-start | bytes 196612
  70.6 4.6 %copy-start.12 = (f32[4,3,64,64]{3,2,1,0:T(8,128)S(1)}, f32[4,3,64,64]{3,2,1,0:T(8,128)}, u32[]{:S(2)}) copy-start(f32[4,3,64,64]{3,2,1,0:T(8,128)} %get-tuple-element.32) | copy-start | bytes 589828
  70.6 4.6 %copy-start.20 = (f32[4,64,64]{2,1,0:T(8,128)S(1)}, f32[4,64,64]{2,1,0:T(8,128)}, u32[]{:S(2)}) copy-start(f32[4,64,64]{2,1,0:T(8,128)} %get-tuple-element.34) | copy-start | bytes 196612
  71.0 4.2 %copy-start.26 = (f32[1,64,64]{2,1,0:T(8,128)S(1)}, f32[1,64,64]{2,1,0:T(8,128)}, u32[]{:S(2)}) copy-start(f32[1,64,64]{2,1,0:T(8,128)} %pad_bitcast_fusion.6) | copy-start | bytes 49156
  71.0 5.3 %copy-start.35 = (s32[16,1]{0,1:T(1,128)S(1)}, s32[16,1]{0,1:T(1,128)}, u32[]{:S(2)}) copy-start(s32[16,1]{0,1:T(1,128)} %stack.37) | copy-start | bytes 196
  71.0 5.3 %copy-start.36 = (s32[16,1]{0,1:T(1,128)S(1)}, s32[16,1]{0,1:T(1,128)}, u32[]{:S(2)}) copy-start(s32[16,1]{0,1:T(1,128)} %stack.38) | copy-start | bytes 196
  71.1 5.3 %copy-start.6 = (f32[4,4,2,4096]{3,2,1,0:T(2,128)S(1)}, f32[4,4,2,4096]{3,2,1,0:T(2,128)}, u32[]{:S(2)}) copy-start(f32[4,4,2,4096]{3,2,1,0:T(2,128)} %copy-done.5) | copy-start | bytes 1572868
  73.4 3.7 %copy-start.31 = (pred[4,4,1]{1,2,0:T(4,128)(4,1)S(1)}, pred[4,4,1]{1,2,0:T(4,128)(4,1)}, u32[]{:S(2)}) copy-start(pred[4,4,1]{1,2,0:T(4,128)(4,1)} %get-tuple-element.46) | copy-start | bytes 52
  73.4 4.3 %copy-start.30 = (pred[4,4,1]{1,2,0:T(4,128)(4,1)S(1)}, pred[4,4,1]{1,2,0:T(4,128)(4,1)}, u32[]{:S(2)}) copy-start(pred[4,4,1]{1,2,0:T(4,128)(4,1)} %get-tuple-element.47) | copy-start | bytes 52
  73.4 4.8 %copy-start.41 = (s32[12]{0:T(128)S(1)}, s32[12]{0:T(128)}, u32[]{:S(2)}) copy-start(s32[12]{0:T(128)} %get-tuple-element.15) | copy-start | bytes 148
  76.3 7.9 %copy-start.14 = (f32[33,64,64]{2,1,0:T(8,128)S(1)}, f32[33,64,64]{2,1,0:T(8,128)}, u32[]{:S(2)}) copy-start(f32[33,64,64]{2,1,0:T(8,128)} %pad_maximum_fusion.5) | copy-start | bytes 1622020
  80.8 23.2 %collective-permute-start.1 = (f32[33,64,64]{2,1,0:T(8,128)}, f32[33,64,64]{2,1,0:T(8,128)}, u32[]{:S(2)}, u32[]{:S(2)}) collective-permute-start(f32[33,64,64]{2,1,0:T(8,128)} %pad_maximum_fusion.3), channel_id=1, source_target_pairs={{1,0},{2,1},{3,2},{4,3},{5,4},{6,5},{7,6},{8,7},{9,8},{10,9},{11,1... | collective-permute-start | bytes 1622024 | tf_op jit(solution)/shard_map/ppermute | solution.py:107
  84.2 28.3 %collective-permute-start.3 = (f32[33,64,64]{2,1,0:T(8,128)S(1)}, f32[33,64,64]{2,1,0:T(8,128)}, u32[]{:S(2)}, u32[]{:S(2)}) collective-permute-start(f32[33,64,64]{2,1,0:T(8,128)S(1)} %copy-done.14), channel_id=1, source_target_pairs={{0,16},{16,32},{32,48},{48,64},{64,80},{80,96},{96,112},{112,128},... | collective-permute-start | bytes 1622024 | tf_op jit(solution)/shard_map/ppermute | solution.py:104
  88.7 30.2 %collective-permute-start.2 = (f32[33,64,64]{2,1,0:T(8,128)}, f32[33,64,64]{2,1,0:T(8,128)S(1)}, u32[]{:S(2)}, u32[]{:S(2)}) collective-permute-start(f32[33,64,64]{2,1,0:T(8,128)} %pad_maximum_fusion.4), channel_id=1, source_target_pairs={{16,0},{32,16},{48,32},{64,48},{80,64},{96,80},{112,96},{128,112},... | collective-permute-start | bytes 1622024 | tf_op jit(solution)/shard_map/ppermute | solution.py:105
  118.9 4.0 %copy-start.15 = (f32[33,64,64]{2,1,0:T(8,128)}, f32[33,64,64]{2,1,0:T(8,128)S(1)}, u32[]{:S(2)}) copy-start(f32[33,64,64]{2,1,0:T(8,128)S(1)} %collective-permute-done.2) | copy-start | bytes 1622020
  119.1 3.8 %copy-start.16 = (f32[4,64,64]{2,1,0:T(8,128)S(1)}, f32[4,64,64]{2,1,0:T(8,128)}, u32[]{:S(2)}) copy-start(f32[4,64,64]{2,1,0:T(8,128)} %copy.262) | copy-start | bytes 196612
  119.1 3.8 %copy-start.17 = (f32[4,64,64]{2,1,0:T(8,128)S(1)}, f32[4,64,64]{2,1,0:T(8,128)}, u32[]{:S(2)}) copy-start(f32[4,64,64]{2,1,0:T(8,128)} %copy.253) | copy-start | bytes 196612
  125.5 7.3 %copy-start.38 = (pred[4,4,1]{1,0,2:T(4,128)(4,1)S(1)}, pred[4,4,1]{1,0,2:T(4,128)(4,1)}, u32[]{:S(2)}) copy-start(pred[4,4,1]{1,0,2:T(4,128)(4,1)} %copy.323) | copy-start | bytes 52
  131.8 1.0 copy-start.27
  132.8 2.1 %copy-start.28 = (f32[4,1,64,64]{3,2,1,0:T(8,128)}, f32[4,1,64,64]{3,2,1,0:T(8,128)S(1)}, u32[]{:S(2)}) copy-start(f32[4,1,64,64]{3,2,1,0:T(8,128)S(1)} %slice_bitcast_fusion.19) | copy-start | bytes 196612
  144.6 9.4 %copy-start.21 = (f32[1,1,2,64,64]{3,4,2,1,0:T(8,128)S(1)}, f32[1,1,2,64,64]{3,4,2,1,0:T(8,128)}, u32[]{:S(2)}) copy-start(f32[1,1,2,64,64]{3,4,2,1,0:T(8,128)} %slice_bitcast_fusion.25) | copy-start | bytes 98308
  144.6 9.4 %copy-start.22 = (f32[1,1,2,64,64]{3,4,2,1,0:T(8,128)S(1)}, f32[1,1,2,64,64]{3,4,2,1,0:T(8,128)}, u32[]{:S(2)}) copy-start(f32[1,1,2,64,64]{3,4,2,1,0:T(8,128)} %slice_bitcast_fusion.24) | copy-start | bytes 98308
  144.6 9.3 %copy-start.23 = (f32[1,1,2,64,64]{3,4,2,1,0:T(8,128)S(1)}, f32[1,1,2,64,64]{3,4,2,1,0:T(8,128)}, u32[]{:S(2)}) copy-start(f32[1,1,2,64,64]{3,4,2,1,0:T(8,128)} %slice_bitcast_fusion.23) | copy-start | bytes 98308
  144.6 9.3 %copy-start.24 = (f32[1,1,2,64,64]{3,4,2,1,0:T(8,128)S(1)}, f32[1,1,2,64,64]{3,4,2,1,0:T(8,128)}, u32[]{:S(2)}) copy-start(f32[1,1,2,64,64]{3,4,2,1,0:T(8,128)} %slice_bitcast_fusion.26) | copy-start | bytes 98308
  154.0 2.1 %copy-start.33 = (pred[8,8]{1,0:T(8,128)(4,1)S(1)}, pred[8,8]{1,0:T(8,128)(4,1)}, u32[]{:S(2)}) copy-start(pred[8,8]{1,0:T(8,128)(4,1)} %get-tuple-element.41) | copy-start | bytes 196
  156.1 2.0 %copy-start.32 = (pred[8,8]{1,0:T(8,128)(4,1)S(1)}, pred[8,8]{1,0:T(8,128)(4,1)}, u32[]{:S(2)}) copy-start(pred[8,8]{1,0:T(8,128)(4,1)} %get-tuple-element.40) | copy-start | bytes 196
  158.1 2.0 %copy-start.2 = (f32[8,8,1,64,64]{4,3,1,0,2:T(8,128)S(1)}, f32[8,8,1,64,64]{4,3,1,0,2:T(8,128)}, u32[]{:S(2)}) copy-start(f32[8,8,1,64,64]{4,3,1,0,2:T(8,128)} %slice_bitcast_fusion.4) | copy-start | bytes 3145732
  166.9 3.0 %copy-start.4 = (f32[36,1,64,64]{2,3,1,0:T(8,128)S(1)}, f32[36,1,64,64]{2,3,1,0:T(8,128)}, u32[]{:S(2)}) copy-start(f32[36,1,64,64]{2,3,1,0:T(8,128)} %copy.282) | copy-start | bytes 1769476
  173.6 6.8 %copy-start.7 = (f32[12,2,64,64]{3,2,1,0:T(8,128)S(1)}, f32[12,2,64,64]{3,2,1,0:T(8,128)}, u32[]{:S(2)}) copy-start(f32[12,2,64,64]{3,2,1,0:T(8,128)} %gather_fusion.2) | copy-start | bytes 1179652
  173.6 6.8 %copy-start.37 = (f32[12]{0:T(128)S(1)}, f32[12]{0:T(128)}, u32[]{:S(2)}) copy-start(f32[12]{0:T(128)} %convert_element_type.240) | copy-start | bytes 148
where the time goes:
time: 195 us; the launch traced here: 193 us
  local copies, waits for them, and re-layouts  88.7 us (45%)
  other arithmetic  40.1 us (21%)
  starting transfers between devices  27.1 us (14%)
  matrix products  22.8 us (12%)
  waiting for transfers between devices  13.2 us (7%)
    dot_general x7, matrix products, matmul(): jnp.einsum('...ij,...jk->...ik', left_block, right_block, precision=PREC)  18 us
    slice x8, local copies, waits for them, and re-layouts, unpack_face(): w_part = buffer[n_p:n_p + n_w]  15.7 us
    ppermute x4, starting transfers between devices, on_device(): lax.ppermute(buffer, ('gx', 'gy'), corner_pairs(n_gx, n_gy, sx, sy))  14.2 us
    ppermute x1, waiting for transfers between devices, on_device(): from_xlo = lax.ppermute(face(high_x, every), 'gx', shift_pairs(n_gx, 1))  7.57 us
    concatenate x4, other arithmetic, face(): jnp.concatenate([fine_own[rows[3], cols[3]].reshape((-1,) + blk), lead_ow...  7.2 us
    gather x1, local copies, waits for them, and re-layouts, on_device(): jnp.take(far.reshape(((nx + 2) * (ny + 2), 7) + blk), picked, axis=0, mod...  6.77 us
    concatenate x4, other arithmetic, on_device(): jnp.concatenate([fine_own[rows2, cols2].reshape((-1,) + blk), lead_own[ro...  6.19 us
    reshape x4, local copies, waits for them, and re-layouts, unpack_corner(): buffer[4:6].reshape((1, 1, 2) + blk)  5.85 us
  transfers between devices with their start and end apart: 8, of which 2 were waited for; matrix products, arithmetic and copies ran while one was open for 34% of the time, Pallas kernels for 0%

commit v1 on v0

--- a/solution.py
+++ b/solution.py
@@ -3,6 +3,8 @@
 import jax
 import jax.numpy as jnp
 from jax import lax
+from jax.experimental import pallas as pl
+from jax.experimental.pallas import tpu as pltpu
 from jax.sharding import PartitionSpec as P
 
 CAP = 12
@@ -60,6 +62,163 @@
     widths = [(1, 0) if before_x else (0, 1), (1, 0) if before_y else (0, 1)]
     widths += [(0, 0)] * (values.ndim - 2)
     return jnp.pad(values, widths)
+
+
+def split(value):
+    high = value.astype(jnp.bfloat16)
+    low = (value - high.astype(jnp.float32)).astype(jnp.bfloat16)
+    return high, low
+
+
+def dot3(left, right, right_t=False):
+    dims = (((1,), (1,)), ((), ())) if right_t else (((1,), (0,)), ((), ()))
+
+    def one(a, b):
+        return lax.dot_general(a, b, dims, preferred_element_type=jnp.float32)
+
+    return one(left[0], right[0]) + one(left[0], right[1]) + one(left[1], right[0])
+
+
+def local_kernel(side_ref, slot_ref, fine_ref, lead_ref, factor_ref, minus_ref,
+                 xlo_ref, xhi_ref, ylo_ref, yhi_ref, cll_ref, clh_ref, chl_ref, chh_ref,
+                 strong_ref, restrict_ref, pg, wg, gg, yg, zg):
+    nx, ny = fine_ref.shape[0], fine_ref.shape[1]
+    blk = fine_ref.shape[2:]
+    zero = jnp.zeros(blk, jnp.float32)
+    wide_x, wide_y = nx + 4, ny + 4
+    pg_src, wg_src, gg_src = {}, {}, {}
+    for i in range(nx):
+        for j in range(ny):
+            pg_src[(3 + i, 3 + j)] = (fine_ref, (i, j))
+            gg_src[(1 + i, 1 + j)] = (factor_ref, (i, j))
+            for e in range(2):
+                wg_src[(2 + i, 2 + j, e)] = (lead_ref, (i, j, e))
+    for c in range(ny):
+        for r in range(3):
+            pg_src[(r, 3 + c)] = (xlo_ref, (r * ny + c,))
+            pg_src[(nx + 3 + r, 3 + c)] = (xhi_ref, (r * ny + c,))
+        for r in range(2):
+            for e in range(2):
+                wg_src[(r, 2 + c, e)] = (xlo_ref, (3 * ny + (r * ny + c) * 2 + e,))
+                wg_src[(nx + 2 + r, 2 + c, e)] = (xhi_ref, (3 * ny + (r * ny + c) * 2 + e,))
+        gg_src[(0, 1 + c)] = (xlo_ref, (7 * ny + c,))
+        gg_src[(nx + 1, 1 + c)] = (xhi_ref, (7 * ny + c,))
+    for i in range(nx):
+        for r in range(3):
+            pg_src[(3 + i, r)] = (ylo_ref, (i * 3 + r,))
+            pg_src[(3 + i, ny + 3 + r)] = (yhi_ref, (i * 3 + r,))
+        for r in range(2):
+            for e in range(2):
+                wg_src[(2 + i, r, e)] = (ylo_ref, (3 * nx + (i * 2 + r) * 2 + e,))
+                wg_src[(2 + i, ny + 2 + r, e)] = (yhi_ref, (3 * nx + (i * 2 + r) * 2 + e,))
+        gg_src[(1 + i, 0)] = (ylo_ref, (7 * nx + i,))
+        gg_src[(1 + i, ny + 1)] = (yhi_ref, (7 * nx + i,))
+    for ref, px, py, wx, wy in ((cll_ref, 1, 1, 1, 1), (clh_ref, 1, ny + 3, 1, ny + 2),
+                                (chl_ref, nx + 3, 1, nx + 2, 1),
+                                (chh_ref, nx + 3, ny + 3, nx + 2, ny + 2)):
+        for a in range(2):
+            for b in range(2):
+                pg_src[(px + a, py + b)] = (ref, (a * 2 + b,))
+        for e in range(2):
+            wg_src[(wx, wy, e)] = (ref, (4 + e,))
+    for i in range(nx + 6):
+        for j in range(ny + 6):
+            ref, at = pg_src.get((i, j), (None, None))
+            pg[i, j] = zero if ref is None else ref[at]
+    for i in range(wide_x):
+        for j in range(wide_y):
+            for e in range(2):
+                ref, at = wg_src.get((i, j, e), (None, None))
+                wg[i, j, e] = zero if ref is None else ref[at]
+    for i in range(nx + 2):
+        for j in range(ny + 2):
+            ref, at = gg_src.get((i, j), (None, None))
+            gg[i, j] = zero if ref is None else ref[at]
+
+    def side(i, j, d):
+        return side_ref[(i * wide_y + j) * 2 + d]
+
+    def near_step(p, carry):
+        i = p // wide_y
+        j = p % wide_y
+        sx = side(i, j, 0)
+        sy = side(i, j, 1)
+        yg[i, j, 0] = dot3(split(wg[i, j, 0]), split(pg[i + 2 * sx, j + 1]))
+        yg[i, j, 1] = dot3(split(wg[i, j, 1]), split(pg[i + 1, j + 2 * sy]))
+        return carry
+
+    lax.fori_loop(0, wide_x * wide_y, near_step, 0)
+
+    def far_step(p, carry):
+        i = p // (ny + 2)
+        j = p % (ny + 2)
+        zg[i, j, 0] = pg[i + 2, j + 2]
+        for e in range(2):
+            s = side(i + 1, j + 1, e)
+            ui = i + 2 * s if e == 0 else i + 1
+            uj = j + 1 if e == 0 else j + 2 * s
+            lead = split(wg[i + 1, j + 1, e])
+            zg[i, j, 1 + 3 * e] = dot3(lead, split(pg[ui + 1, uj + 1]))
+            zg[i, j, 2 + 3 * e] = dot3(lead, split(yg[ui, uj, 0]))
+            zg[i, j, 3 + 3 * e] = dot3(lead, split(yg[ui, uj, 1]))
+        return carry
+
+    lax.fori_loop(0, (nx + 2) * (ny + 2), far_step, 0)
+
+    def strong_step(p, carry):
+        i = p // ny
+        j = p % ny
+        factor = split(factor_ref[i, j])
+        for d in range(2):
+            s = side(i + 2, j + 2, d)
+            up = gg[i + 2 * s, j + 1] if d == 0 else gg[i + 1, j + 2 * s]
+            scaled = dot3(split(dot3(factor, split(minus_ref[i, j, d]))), split(up), True)
+            total = jnp.sum(scaled * scaled, axis=(0, 1), keepdims=True)
+            strong_ref[p * 2 + d] = jnp.broadcast_to(total * (1.0 / scaled.size), (1, 128))
+        return carry
+
+    lax.fori_loop(0, nx * ny, strong_step, 0)
+
+    def slot_step(s, carry):
+        cell = slot_ref[s * 4]
+        weight = slot_ref[s * 4 + 3].astype(jnp.float32)
+        ci = cell // ny
+        cj = cell % ny
+        for d in range(2):
+            n = slot_ref[s * 4 + 1 + d]
+            ni = n // (ny + 2)
+            nj = n % (ny + 2)
+            coupling = split(minus_ref[ci, cj, d])
+            for w in range(7):
+                row = dot3(coupling, split(zg[ni, nj, w]))
+                restrict_ref[s, d * 7 + w] = (row * weight).astype(restrict_ref.dtype)
+        return carry
+
+    lax.fori_loop(0, restrict_ref.shape[0], slot_step, 0)
+
+
+def local_compute(side_flat, slot_table, fine_own, lead_own, factor_own, minus_own, buffers):
+    nx, ny = fine_own.shape[:2]
+    blk = fine_own.shape[2:]
+    vmem = pl.BlockSpec(memory_space=pltpu.VMEM)
+    smem = pl.BlockSpec(memory_space=pltpu.SMEM)
+    f32 = jnp.float32
+    strong, restrict = pl.pallas_call(
+        local_kernel,
+        out_shape=(jax.ShapeDtypeStruct((nx * ny * 2, 1, 128), f32),
+                   jax.ShapeDtypeStruct((CAP, 14) + blk, jnp.bfloat16)),
+        in_specs=[smem, smem] + [vmem] * (4 + len(buffers)),
+        out_specs=(vmem, vmem),
+        scratch_shapes=[
+            pltpu.VMEM((nx + 6, ny + 6) + blk, f32),
+            pltpu.VMEM((nx + 4, ny + 4, 2) + blk, f32),
+            pltpu.VMEM((nx + 2, ny + 2) + blk, f32),
+            pltpu.VMEM((nx + 4, ny + 4, 2) + blk, f32),
+            pltpu.VMEM((nx + 2, ny + 2, 7) + blk, f32),
+        ],
+        compiler_params=pltpu.CompilerParams(vmem_limit_bytes=60 * 1024 * 1024),
+    )(side_flat, slot_table, fine_own, lead_own, factor_own, minus_own, *buffers)
+    return strong[:, 0, 0].reshape(nx, ny, 2), restrict
 
 
 def on_device(inv_factors, couplings, stencil, coarse):
@@ -161,43 +320,7 @@
             axis=0,
         )
 
-    fine_cycle = cycle(0, pxl, fine_own, pxh, pyl, pyh)
-    lead_cycle = cycle(1, wxl, lead_own, wxh, wyl, wyh)
     side_cycle = cycle(2, cxl, stencil, cxh, cyl, cyh)
-    corner_zero = jnp.zeros((1, 1) + blk, jnp.float32)
-    factor_cycle = jnp.concatenate(
-        [
-            row_band([corner_zero, gxl, corner_zero]),
-            row_band([gyl, factor_own, gyh]),
-            row_band([corner_zero, gxh, corner_zero]),
-        ],
-        axis=0,
-    )
-
-    up_x, up_y = upwind_pick(fine_cycle, side_cycle)
-    near = jnp.stack(
-        [crop_cycle(fine_cycle, 1), matmul(lead_cycle[:, :, 0], up_x),
-         matmul(lead_cycle[:, :, 1], up_y)],
-        axis=2,
-    )
-    near_x, near_y = upwind_pick(near, crop_cycle(side_cycle, 1))
-    lead_6 = crop_cycle(lead_cycle, 1)
-    far = jnp.concatenate(
-        [
-            crop_cycle(fine_cycle, 2)[:, :, None],
-            matmul(lead_6[:, :, 0:1], near_x),
-            matmul(lead_6[:, :, 1:2], near_y),
-        ],
-        axis=2,
-    )
-
-    gup_x, gup_y = upwind_pick(factor_cycle, stencil)
-    scaled_left = matmul(factor_own[:, :, None], minus_own)
-    strong = []
-    for direction, gup in ((0, gup_x), (1, gup_y)):
-        scaled = right_gram(scaled_left[:, :, direction], gup)
-        strong.append(jnp.mean(scaled * scaled, axis=(-2, -1)))
-    strong = jnp.stack(strong, axis=-1)
 
     cell_count = nx * ny
     flat_coarse = coarse.reshape(cell_count)
@@ -218,15 +341,12 @@
          own_i * span + own_j + 2 * stencil[:, :, 1] - 1],
         axis=-1,
     ).reshape(cell_count, 2)
-    picked = jnp.take(up_index, source, axis=0, mode="clip").reshape(CAP * 2)
-    far_rows = jnp.take(far.reshape(((nx + 2) * (ny + 2), 7) + blk), picked, axis=0,
-                        mode="clip").reshape((CAP, 2, 7) + blk)
-    coupling_rows = jnp.take(minus_own.reshape((cell_count, 2) + blk), source, axis=0,
-                             mode="clip")
-    restrict = matmul(coupling_rows[:, :, None], far_rows)
-    restrict = (restrict * filled[:, None, None, None, None].astype(restrict.dtype)).astype(
-        jnp.bfloat16
-    )
+    picked = jnp.take(up_index, source, axis=0, mode="clip")
+    slot_table = jnp.concatenate([source[:, None], picked, filled[:, None]], axis=1).reshape(-1)
+    buffers = (from_xlo, from_xhi, from_ylo, from_yhi, corners[(1, 1)], corners[(1, -1)],
+               corners[(-1, 1)], corners[(-1, -1)])
+    strong, restrict = local_compute(side_cycle.reshape(-1), slot_table, fine_own, lead_own,
+                                     factor_own, minus_own, buffers)
     return (strong, restrict.reshape(CAP, 14, flat))
 
 

time: 195 us -> 125 us (0.64)
  the two profiles are of different devices: /device:TPU:120 before, /device:TPU:103 now
where the time goes in v1:
time: 125 us; the launch traced here: 124 us
  Pallas kernels  35.7 us (29%)
  starting transfers between devices  31 us (25%)
  local copies, waits for them, and re-layouts  23 us (18%)
  other arithmetic  17.5 us (14%)
  waiting for transfers between devices  15.2 us (12%)
    pallas_call x1, Pallas kernels, local_compute(): pl.pallas_call(local_kernel, out_shape=(jax.ShapeDtypeStruct((nx * ny * 2...  35.7 us
    ppermute x4, starting transfers between devices, on_device(): lax.ppermute(buffer, ('gx', 'gy'), corner_pairs(n_gx, n_gy, sx, sy))  17.6 us
    ppermute x1, waiting for transfers between devices, on_device(): from_xlo = lax.ppermute(face(high_x, every), 'gx', shift_pairs(n_gx, 1))  15.1 us
    concatenate x4, other arithmetic, face(): jnp.concatenate([fine_own[rows[3], cols[3]].reshape((-1,) + blk), lead_ow...  6.53 us
    reshape x1, local copies, waits for them, and re-layouts, on_device(): return (strong, restrict.reshape(CAP, 14, flat))  5.02 us
    ppermute x1, starting transfers between devices, on_device(): from_ylo = lax.ppermute(face(every, high_y), 'gy', shift_pairs(n_gy, 1))  4.84 us
    ppermute x1, starting transfers between devices, on_device(): from_xhi = lax.ppermute(face(low, every), 'gx', shift_pairs(n_gx, -1))  4.73 us
    reshape x3, local copies, waits for them, and re-layouts, face(): factor_own[rows[1], cols[1]].reshape((-1,) + blk)  3.32 us
  transfers between devices with their start and end apart: 8, of which 1 were waited for; matrix products, arithmetic and copies ran while one was open for 21% of the time, Pallas kernels for 0%

profile of v1, /device:TPU:103, one launch (start us, length us, event | category | flops | bytes accessed | tf_op | source)
XLA Modules:
  0.0 124.5 jit_solution(3413902137021141938)
XLA Ops:
  0.6 0.7 subtract_convert_fusion
  1.4 1.0 convert_reduce_fusion.4
  2.4 0.8 compare_and_fusion.1
  3.2 0.1 copy.103
  3.4 1.1 copy.100
  4.5 0.3 reshape.347
  4.8 0.3 broadcast_multiply_fusion
  5.1 0.6 reshape.349.minus_ref
  5.7 0.6 convolution_multiply_fusion.fine_ref
  6.4 0.6 convolution_bitcast_fusion.lead_ref
  7.0 0.7 pad_maximum_fusion.5
  7.7 3.8 %collective-permute-start.2 = (f32[7,64,64]{2,1,0:T(8,128)}, f32[7,64,64]{2,1,0:T(8,128)}, u32[]{:S(2)}, u32[]{:S(2)}) collective-permute-start(f32[7,64,64]{2,1,0:T(8,128)} %pad_maximum_fusion.5), channel_id=1, source_target_pairs={{1,16},{2,17},{3,18},{4,19},{5,20},{6,21},{7,22},{8,23},{9,24},{10... | collective-permute-start | bytes 344072 | tf_op jit(solution)/shard_map/ppermute | solution.py:283
  11.5 0.7 pad_maximum_fusion.6
  12.2 6.2 %collective-permute-start.5 = (f32[7,64,64]{2,1,0:T(8,128)}, f32[7,64,64]{2,1,0:T(8,128)}, u32[]{:S(2)}, u32[]{:S(2)}) collective-permute-start(f32[7,64,64]{2,1,0:T(8,128)} %pad_maximum_fusion.6), channel_id=1, source_target_pairs={{16,1},{17,2},{18,3},{19,4},{20,5},{21,6},{22,7},{23,8},{24,9},{25... | collective-permute-start | bytes 344072 | tf_op jit(solution)/shard_map/ppermute | solution.py:283
  18.4 0.7 pad_maximum_fusion.7
  19.1 1.9 %collective-permute-start.7 = (f32[7,64,64]{2,1,0:T(8,128)}, f32[7,64,64]{2,1,0:T(8,128)}, u32[]{:S(2)}, u32[]{:S(2)}) collective-permute-start(f32[7,64,64]{2,1,0:T(8,128)} %pad_maximum_fusion.7), channel_id=1, source_target_pairs={{17,0},{18,1},{19,2},{20,3},{21,4},{22,5},{23,6},{24,7},{25,8},{26... | collective-permute-start | bytes 344072 | tf_op jit(solution)/shard_map/ppermute | solution.py:283
  21.0 0.7 pad_maximum_fusion.4
  21.8 5.7 %collective-permute-start = (f32[7,64,64]{2,1,0:T(8,128)}, f32[7,64,64]{2,1,0:T(8,128)}, u32[]{:S(2)}, u32[]{:S(2)}) collective-permute-start(f32[7,64,64]{2,1,0:T(8,128)} %pad_maximum_fusion.4), channel_id=1, source_target_pairs={{0,17},{1,18},{2,19},{3,20},{4,21},{5,22},{6,23},{7,24},{8,25},{9,... | collective-permute-start | bytes 344072 | tf_op jit(solution)/shard_map/ppermute | solution.py:283
  27.5 0.6 slice_convert_fusion.1
  28.1 0.7 fusion.15
  28.8 0.8 fusion.12
  29.6 0.1 fusion.10
  29.9 0.6 pad_bitcast_fusion.1
  30.5 1.6 %reshape.363 = f32[4,64,64]{2,1,0:T(8,128)} reshape(f32[1,4,4096]{2,1,0:T(4,128)} %get-tuple-element.43) | data formatting | bytes 131072 | tf_op jit(solution)/shard_map/reshape | solution.py:253
  32.1 2.2 %pad_maximum_fusion.3 = f32[33,64,64]{2,1,0:T(8,128)} fusion(f32[1,64,64]{2,1,0:T(8,128)} %pad_bitcast_fusion.1, f32[4,64,64]{2,1,0:T(8,128)} %reshape.363, f32[16,64,64]{2,1,0:T(8,128)S(1)} %bitcast.61, f32[12,64,64]{2,1,0:T(8,128)} %bitcast.65), kind=kLoop, calls=%fused_computation.6 | loop fusion | flops 405504 | bytes 1081344 | tf_op jit(solution)/shard_map/concatenate | solution.py:249
  34.3 4.7 %collective-permute-start.6 = (f32[33,64,64]{2,1,0:T(8,128)}, f32[33,64,64]{2,1,0:T(8,128)}, u32[]{:S(2)}, u32[]{:S(2)}) collective-permute-start(f32[33,64,64]{2,1,0:T(8,128)} %pad_maximum_fusion.3), channel_id=1, source_target_pairs={{16,0},{32,16},{48,32},{64,48},{80,64},{96,80},{112,96},{128,112},... | collective-permute-start | bytes 1622024 | tf_op jit(solution)/shard_map/ppermute | solution.py:264
  39.0 0.6 reshape.368
  39.6 0.6 iota_add_fusion
  40.3 0.7 fusion.16
  40.9 0.7 slice_bitcast_fusion.1
  41.7 0.9 copy.127.factor_ref
  42.5 0.8 fusion.13
  43.4 0.1 fusion.11
  43.5 0.5 copy-done.14
  44.6 0.1 reduce.8
  44.8 0.1 select_reduce_fusion
  45.1 0.6 gather_fusion
  45.7 0.6 reshape.369.slot_ref
  46.5 0.1 copy.111
  46.8 0.1 copy.113
  47.0 1.0 reshape.352
  48.0 2.2 %pad_maximum_fusion.1 = f32[33,64,64]{2,1,0:T(8,128)} fusion(f32[1,64,64]{2,1,0:T(8,128)S(1)} %pad_bitcast_fusion.4, f32[4,64,64]{2,1,0:T(8,128)} %get-tuple-element.36, f32[16,64,64]{2,1,0:T(8,128)S(1)} %bitcast.60, f32[12,64,64]{2,1,0:T(8,128)} %bitcast.64), kind=kLoop, calls=%fused_computation.4 | loop fusion | flops 405504 | bytes 1081344 | tf_op jit(solution)/shard_map/concatenate | solution.py:249
  50.1 1.1 pad_maximum_fusion.2
  51.2 1.1 pad_maximum_fusion
  52.3 1.9 %collective-permute-start.1 = (f32[33,64,64]{2,1,0:T(8,128)}, f32[33,64,64]{2,1,0:T(8,128)S(1)}, u32[]{:S(2)}, u32[]{:S(2)}) collective-permute-start(f32[33,64,64]{2,1,0:T(8,128)} %pad_maximum_fusion), channel_id=1, source_target_pairs={{0,16},{16,32},{32,48},{48,64},{64,80},{80,96},{96,112},{112,128},... | collective-permute-start | bytes 1622024 | tf_op jit(solution)/shard_map/ppermute | solution.py:263
  54.3 0.7 slice_convert_fusion.7
  54.9 1.9 %collective-permute-start.4 = (f32[33,64,64]{2,1,0:T(8,128)}, f32[33,64,64]{2,1,0:T(8,128)S(1)}, u32[]{:S(2)}, u32[]{:S(2)}) collective-permute-start(f32[33,64,64]{2,1,0:T(8,128)} %pad_maximum_fusion.2), channel_id=1, source_target_pairs={{1,0},{2,1},{3,2},{4,3},{5,4},{6,5},{7,6},{8,7},{9,8},{10,9},{11,1... | collective-permute-start | bytes 1622024 | tf_op jit(solution)/shard_map/ppermute | solution.py:266
  56.9 0.7 slice_convert_fusion.4
  57.5 4.8 %collective-permute-start.3 = (f32[33,64,64]{2,1,0:T(8,128)}, f32[33,64,64]{2,1,0:T(8,128)S(1)}, u32[]{:S(2)}, u32[]{:S(2)}) collective-permute-start(f32[33,64,64]{2,1,0:T(8,128)} %pad_maximum_fusion.1), channel_id=1, source_target_pairs={{0,1},{1,2},{2,3},{3,4},{4,5},{5,6},{6,7},{7,8},{8,9},{9,10},{10,1... | collective-permute-start | bytes 1622024 | tf_op jit(solution)/shard_map/ppermute | solution.py:265
  62.4 0.7 slice_convert_fusion.2
  63.4 0.7 slice_convert_fusion.9
  64.1 0.7 fusion.5
  64.9 0.1 copy.118
  65.0 15.1 %collective-permute-done.1.xlo_ref = f32[33,64,64]{2,1,0:T(8,128)S(1)} collective-permute-done((f32[33,64,64]{2,1,0:T(8,128)}, f32[33,64,64]{2,1,0:T(8,128)S(1)}, u32[]{:S(2)}, u32[]{:S(2)}) %collective-permute-start.1) | collective-permute-done | bytes 540704 | tf_op jit(solution)/shard_map/ppermute | solution.py:263
  80.3 0.1 copy.108
  80.5 0.1 copy.115
  80.7 0.1 copy.114
  80.9 0.1 copy.120
  81.1 0.7 reshape.365.side_ref
  81.7 0.1 copy-done.5
  81.9 35.7 %shard_map.59 = (f32[32,1,128]{2,1,0:T(1,128)}, bf16[12,14,64,64]{3,2,1,0:T(8,128)(2,1)}) custom-call(s32[128]{0:T(128)} %reshape.365.side_ref, s32[48]{0:T(128)} %reshape.369.slot_ref, f32[4,4,64,64]{3,2,1,0:T(8,128)} %copy-done, f32[4,4,2,64,64]{4,3,2,1,0:T(8,128)} %copy-done.1, f32[4,4,64,64]{3,2,1,0:T(8,128)} %copy.127.factor_ref, ...), custom_call_target="tpu_custom_call" | custom-call | tf_op jit(solution)/shard_map/pallas_call | solution.py:206
  117.6 1.0 slice_reduce_fusion
  118.8 0.7 copy.126
  119.5 5.0 %reshape.370 = bf16[12,14,4096]{2,1,0:T(8,128)(2,1)} reshape(bf16[12,14,64,64]{3,2,1,0:T(8,128)(2,1)} %get-tuple-element.5) | data formatting | bytes 2752512 | tf_op jit(solution)/shard_map/reshape | solution.py:350
  (84 shorter events, 2.7 us)
Async XLA Ops:
  0.6 4.1 %copy-start.7 = (f32[4,4,2,4096]{3,2,1,0:T(2,128)S(1)}, f32[4,4,2,4096]{3,2,1,0:T(2,128)}, u32[]{:S(2)}) copy-start(f32[4,4,2,4096]{3,2,1,0:T(2,128)} %param.5) | copy-start | bytes 1572868
  5.7 1.2 copy-start.2
  6.3 36.3 %copy-start = (f32[4,4,64,64]{3,2,1,0:T(8,128)}, f32[4,4,64,64]{3,2,1,0:T(8,128)S(1)}, u32[]{:S(2)}) copy-start(f32[4,4,64,64]{3,2,1,0:T(8,128)S(1)} %convolution_multiply_fusion.fine_ref) | copy-start | bytes 786436
  6.9 36.5 %copy-start.1 = (f32[4,4,2,64,64]{4,3,2,1,0:T(8,128)}, f32[4,4,2,64,64]{4,3,2,1,0:T(8,128)S(1)}, u32[]{:S(2)}) copy-start(f32[4,4,2,64,64]{4,3,2,1,0:T(8,128)S(1)} %convolution_bitcast_fusion.lead_ref) | copy-start | bytes 1572868
  7.0 20.5 %copy-start.9 = (s32[4,4,2]{1,2,0:T(2,128)S(1)}, s32[4,4,2]{1,2,0:T(2,128)}, u32[]{:S(2)}) copy-start(s32[4,4,2]{1,2,0:T(2,128)} %param.6) | copy-start | bytes 388
  7.0 21.1 %copy-start.6 = (f32[4,4,4096]{2,1,0:T(4,128)S(1)}, f32[4,4,4096]{2,1,0:T(4,128)}, u32[]{:S(2)}) copy-start(f32[4,4,4096]{2,1,0:T(4,128)} %param.4) | copy-start | bytes 786436
  7.7 44.6 %collective-permute-start.2 = (f32[7,64,64]{2,1,0:T(8,128)}, f32[7,64,64]{2,1,0:T(8,128)}, u32[]{:S(2)}, u32[]{:S(2)}) collective-permute-start(f32[7,64,64]{2,1,0:T(8,128)} %pad_maximum_fusion.5), channel_id=1, source_target_pairs={{1,16},{2,17},{3,18},{4,19},{5,20},{6,21},{7,22},{8,23},{9,24},{10... | collective-permute-start | bytes 344072 | tf_op jit(solution)/shard_map/ppermute | solution.py:283
  12.2 42.7 %collective-permute-start.5 = (f32[7,64,64]{2,1,0:T(8,128)}, f32[7,64,64]{2,1,0:T(8,128)}, u32[]{:S(2)}, u32[]{:S(2)}) collective-permute-start(f32[7,64,64]{2,1,0:T(8,128)} %pad_maximum_fusion.6), channel_id=1, source_target_pairs={{16,1},{17,2},{18,3},{19,4},{20,5},{21,6},{22,7},{23,8},{24,9},{25... | collective-permute-start | bytes 344072 | tf_op jit(solution)/shard_map/ppermute | solution.py:283
  19.1 38.4 %collective-permute-start.7 = (f32[7,64,64]{2,1,0:T(8,128)}, f32[7,64,64]{2,1,0:T(8,128)}, u32[]{:S(2)}, u32[]{:S(2)}) collective-permute-start(f32[7,64,64]{2,1,0:T(8,128)} %pad_maximum_fusion.7), channel_id=1, source_target_pairs={{17,0},{18,1},{19,2},{20,3},{21,4},{22,5},{23,6},{24,7},{25,8},{26... | collective-permute-start | bytes 344072 | tf_op jit(solution)/shard_map/ppermute | solution.py:283
  21.8 41.6 %collective-permute-start = (f32[7,64,64]{2,1,0:T(8,128)}, f32[7,64,64]{2,1,0:T(8,128)}, u32[]{:S(2)}, u32[]{:S(2)}) collective-permute-start(f32[7,64,64]{2,1,0:T(8,128)} %pad_maximum_fusion.4), channel_id=1, source_target_pairs={{0,17},{1,18},{2,19},{3,20},{4,21},{5,22},{6,23},{7,24},{8,25},{9,... | collective-permute-start | bytes 344072 | tf_op jit(solution)/shard_map/ppermute | solution.py:283
  32.1 6.9 %copy-start.10 = (s32[4,4]{1,0:T(4,128)S(1)}, s32[4,4]{1,0:T(4,128)}, u32[]{:S(2)}) copy-start(s32[4,4]{1,0:T(4,128)} %param.7) | copy-start | bytes 196
  34.3 29.8 %collective-permute-start.6 = (f32[33,64,64]{2,1,0:T(8,128)}, f32[33,64,64]{2,1,0:T(8,128)}, u32[]{:S(2)}, u32[]{:S(2)}) collective-permute-start(f32[33,64,64]{2,1,0:T(8,128)} %pad_maximum_fusion.3), channel_id=1, source_target_pairs={{16,0},{32,16},{48,32},{64,48},{80,64},{96,80},{112,96},{128,112},... | collective-permute-start | bytes 1622024 | tf_op jit(solution)/shard_map/ppermute | solution.py:264
  43.4 0.6 copy-start.14
  43.4 0.7 copy-start.13
  43.4 0.7 copy-start.15
  43.4 0.9 copy-start.12
  43.4 3.0 %copy-start.11 = (s32[4,2,2]{1,2,0:T(2,128)S(1)}, s32[4,2,2]{1,2,0:T(2,128)}, u32[]{:S(2)}) copy-start(s32[4,2,2]{1,2,0:T(2,128)} %get-tuple-element.46) | copy-start | bytes 196
  48.0 2.2 %copy-start.8 = (f32[4,64,64]{2,1,0:T(8,128)S(1)}, f32[4,64,64]{2,1,0:T(8,128)}, u32[]{:S(2)}) copy-start(f32[4,64,64]{2,1,0:T(8,128)} %get-tuple-element.37) | copy-start | bytes 196612
  52.3 27.8 %collective-permute-start.1 = (f32[33,64,64]{2,1,0:T(8,128)}, f32[33,64,64]{2,1,0:T(8,128)S(1)}, u32[]{:S(2)}, u32[]{:S(2)}) collective-permute-start(f32[33,64,64]{2,1,0:T(8,128)} %pad_maximum_fusion), channel_id=1, source_target_pairs={{0,16},{16,32},{32,48},{48,64},{64,80},{80,96},{96,112},{112,128},... | collective-permute-start | bytes 1622024 | tf_op jit(solution)/shard_map/ppermute | solution.py:263
  54.9 25.4 %collective-permute-start.4 = (f32[33,64,64]{2,1,0:T(8,128)}, f32[33,64,64]{2,1,0:T(8,128)S(1)}, u32[]{:S(2)}, u32[]{:S(2)}) collective-permute-start(f32[33,64,64]{2,1,0:T(8,128)} %pad_maximum_fusion.2), channel_id=1, source_target_pairs={{1,0},{2,1},{3,2},{4,3},{5,4},{6,5},{7,6},{8,7},{9,8},{10,9},{11,1... | collective-permute-start | bytes 1622024 | tf_op jit(solution)/shard_map/ppermute | solution.py:266
  57.5 23.1 %collective-permute-start.3 = (f32[33,64,64]{2,1,0:T(8,128)}, f32[33,64,64]{2,1,0:T(8,128)S(1)}, u32[]{:S(2)}, u32[]{:S(2)}) collective-permute-start(f32[33,64,64]{2,1,0:T(8,128)} %pad_maximum_fusion.1), channel_id=1, source_target_pairs={{0,1},{1,2},{2,3},{3,4},{4,5},{5,6},{6,7},{7,8},{8,9},{9,10},{10,1... | collective-permute-start | bytes 1622024 | tf_op jit(solution)/shard_map/ppermute | solution.py:265
  80.2 1.6 %copy-start.3 = (f32[33,64,64]{2,1,0:T(8,128)}, f32[33,64,64]{2,1,0:T(8,128)S(1)}, u32[]{:S(2)}) copy-start(f32[33,64,64]{2,1,0:T(8,128)S(1)} %collective-permute-done.1.xlo_ref) | copy-start | bytes 1622020
  80.4 1.4 %copy-start.4 = (f32[33,64,64]{2,1,0:T(8,128)}, f32[33,64,64]{2,1,0:T(8,128)S(1)}, u32[]{:S(2)}) copy-start(f32[33,64,64]{2,1,0:T(8,128)S(1)} %collective-permute-done.4.yhi_ref) | copy-start | bytes 1622020
  80.6 1.3 %copy-start.5 = (f32[33,64,64]{2,1,0:T(8,128)}, f32[33,64,64]{2,1,0:T(8,128)S(1)}, u32[]{:S(2)}) copy-start(f32[33,64,64]{2,1,0:T(8,128)S(1)} %collective-permute-done.3.ylo_ref) | copy-start | bytes 1622020

commit v2 on v1

--- a/solution.py
+++ b/solution.py
@@ -147,7 +147,7 @@
         yg[i, j, 1] = dot3(split(wg[i, j, 1]), split(pg[i + 1, j + 2 * sy]))
         return carry
 
-    lax.fori_loop(0, wide_x * wide_y, near_step, 0)
+    lax.fori_loop(0, wide_x * wide_y, near_step, 0, unroll=4)
 
     def far_step(p, carry):
         i = p // (ny + 2)
@@ -163,7 +163,7 @@
             zg[i, j, 3 + 3 * e] = dot3(lead, split(yg[ui, uj, 1]))
         return carry
 
-    lax.fori_loop(0, (nx + 2) * (ny + 2), far_step, 0)
+    lax.fori_loop(0, (nx + 2) * (ny + 2), far_step, 0, unroll=4)
 
     def strong_step(p, carry):
         i = p // ny
@@ -177,7 +177,7 @@
             strong_ref[p * 2 + d] = jnp.broadcast_to(total * (1.0 / scaled.size), (1, 128))
         return carry
 
-    lax.fori_loop(0, nx * ny, strong_step, 0)
+    lax.fori_loop(0, nx * ny, strong_step, 0, unroll=4)
 
     def slot_step(s, carry):
         cell = slot_ref[s * 4]
@@ -194,7 +194,7 @@
                 restrict_ref[s, d * 7 + w] = (row * weight).astype(restrict_ref.dtype)
         return carry
 
-    lax.fori_loop(0, restrict_ref.shape[0], slot_step, 0)
+    lax.fori_loop(0, restrict_ref.shape[0], slot_step, 0, unroll=4)
 
 
 def local_compute(side_flat, slot_table, fine_own, lead_own, factor_own, minus_own, buffers):

time: 125 us -> 110 us (0.88)
  Pallas kernels: 35.7 us -> 20.4 us
    pallas_call x1, Pallas kernels: 35.7 us -> 20.4 us  [local_compute(): pl.pallas_call(local_kernel, out_shape=(jax.ShapeDtypeStruct((nx * ny * 2...]
  transfers between devices with their start and end apart: 8 -> 8, of which waited for: 1 -> 1; matrix products, arithmetic and copies ran while one was open for 21% -> 24% of each run, Pallas kernels for 0% -> 0%
where the time goes in v2:
time: 110 us; the launch traced here: 109 us
  starting transfers between devices  31 us (28%)
  local copies, waits for them, and re-layouts  23 us (21%)
  Pallas kernels  20.4 us (19%)
  other arithmetic  17.5 us (16%)
  waiting for transfers between devices  15.2 us (14%)
  matrix products  1.15 us (1%)
    pallas_call x1, Pallas kernels, local_compute(): pl.pallas_call(local_kernel, out_shape=(jax.ShapeDtypeStruct((nx * ny * 2...  20.4 us
    ppermute x4, starting transfers between devices, on_device(): lax.ppermute(buffer, ('gx', 'gy'), corner_pairs(n_gx, n_gy, sx, sy))  17.6 us
    ppermute x1, waiting for transfers between devices, on_device(): from_xlo = lax.ppermute(face(high_x, every), 'gx', shift_pairs(n_gx, 1))  15.1 us
    concatenate x4, other arithmetic, face(): jnp.concatenate([fine_own[rows[3], cols[3]].reshape((-1,) + blk), lead_ow...  6.53 us
    reshape x1, local copies, waits for them, and re-layouts, on_device(): return (strong, restrict.reshape(CAP, 14, flat))  5.02 us
    ppermute x1, starting transfers between devices, on_device(): from_ylo = lax.ppermute(face(every, high_y), 'gy', shift_pairs(n_gy, 1))  4.84 us
    ppermute x1, starting transfers between devices, on_device(): from_xhi = lax.ppermute(face(low, every), 'gx', shift_pairs(n_gx, -1))  4.73 us
    reshape x3, local copies, waits for them, and re-layouts, face(): factor_own[rows[1], cols[1]].reshape((-1,) + blk)  3.32 us
  transfers between devices with their start and end apart: 8, of which 1 were waited for; matrix products, arithmetic and copies ran while one was open for 24% of the time, Pallas kernels for 0%

profile of v2, /device:TPU:103, one launch (start us, length us, event | category | flops | bytes accessed | tf_op | source)
XLA Modules:
  0.0 109.1 jit_solution(6331477892799898808)
XLA Ops:
  0.6 0.7 subtract_convert_fusion
  1.4 1.0 convert_reduce_fusion.4
  2.4 0.8 compare_and_fusion.1
  3.2 0.1 copy.103
  3.4 1.1 %copy.100 = f32[4,4,4096]{2,0,1:T(4,128)S(1)} copy(f32[4,4,4096]{2,1,0:T(4,128)} %param.4) | data formatting | bytes 524288 | tf_op args[0]
  4.5 0.3 reshape.347
  4.8 0.3 broadcast_multiply_fusion
  5.1 0.6 reshape.349.minus_ref
  5.7 0.6 convolution_multiply_fusion.fine_ref
  6.4 0.6 convolution_bitcast_fusion.lead_ref
  7.0 0.7 pad_maximum_fusion.5
  7.7 3.8 %collective-permute-start.2 = (f32[7,64,64]{2,1,0:T(8,128)}, f32[7,64,64]{2,1,0:T(8,128)}, u32[]{:S(2)}, u32[]{:S(2)}) collective-permute-start(f32[7,64,64]{2,1,0:T(8,128)} %pad_maximum_fusion.5), channel_id=1, source_target_pairs={{1,16},{2,17},{3,18},{4,19},{5,20},{6,21},{7,22},{8,23},{9,24},{10... | collective-permute-start | bytes 344072 | tf_op jit(solution)/shard_map/ppermute | solution.py:283
  11.5 0.7 pad_maximum_fusion.6
  12.2 6.2 %collective-permute-start.5 = (f32[7,64,64]{2,1,0:T(8,128)}, f32[7,64,64]{2,1,0:T(8,128)}, u32[]{:S(2)}, u32[]{:S(2)}) collective-permute-start(f32[7,64,64]{2,1,0:T(8,128)} %pad_maximum_fusion.6), channel_id=1, source_target_pairs={{16,1},{17,2},{18,3},{19,4},{20,5},{21,6},{22,7},{23,8},{24,9},{25... | collective-permute-start | bytes 344072 | tf_op jit(solution)/shard_map/ppermute | solution.py:283
  18.4 0.7 pad_maximum_fusion.7
  19.1 1.9 %collective-permute-start.7 = (f32[7,64,64]{2,1,0:T(8,128)}, f32[7,64,64]{2,1,0:T(8,128)}, u32[]{:S(2)}, u32[]{:S(2)}) collective-permute-start(f32[7,64,64]{2,1,0:T(8,128)} %pad_maximum_fusion.7), channel_id=1, source_target_pairs={{17,0},{18,1},{19,2},{20,3},{21,4},{22,5},{23,6},{24,7},{25,8},{26... | collective-permute-start | bytes 344072 | tf_op jit(solution)/shard_map/ppermute | solution.py:283
  21.0 0.7 pad_maximum_fusion.4
  21.8 5.7 %collective-permute-start = (f32[7,64,64]{2,1,0:T(8,128)}, f32[7,64,64]{2,1,0:T(8,128)}, u32[]{:S(2)}, u32[]{:S(2)}) collective-permute-start(f32[7,64,64]{2,1,0:T(8,128)} %pad_maximum_fusion.4), channel_id=1, source_target_pairs={{0,17},{1,18},{2,19},{3,20},{4,21},{5,22},{6,23},{7,24},{8,25},{9,... | collective-permute-start | bytes 344072 | tf_op jit(solution)/shard_map/ppermute | solution.py:283
  27.5 0.6 slice_convert_fusion.1
  28.1 0.7 fusion.15
  28.8 0.8 fusion.12
  29.6 0.1 fusion.10
  29.9 0.6 pad_bitcast_fusion.1
  30.5 1.6 %reshape.363 = f32[4,64,64]{2,1,0:T(8,128)} reshape(f32[1,4,4096]{2,1,0:T(4,128)} %get-tuple-element.43) | data formatting | bytes 131072 | tf_op jit(solution)/shard_map/reshape | solution.py:253
  32.1 2.2 %pad_maximum_fusion.3 = f32[33,64,64]{2,1,0:T(8,128)} fusion(f32[1,64,64]{2,1,0:T(8,128)} %pad_bitcast_fusion.1, f32[4,64,64]{2,1,0:T(8,128)} %reshape.363, f32[16,64,64]{2,1,0:T(8,128)S(1)} %bitcast.61, f32[12,64,64]{2,1,0:T(8,128)} %bitcast.65), kind=kLoop, calls=%fused_computation.6 | loop fusion | flops 405504 | bytes 1081344 | tf_op jit(solution)/shard_map/concatenate | solution.py:249
  34.3 4.7 %collective-permute-start.6 = (f32[33,64,64]{2,1,0:T(8,128)}, f32[33,64,64]{2,1,0:T(8,128)}, u32[]{:S(2)}, u32[]{:S(2)}) collective-permute-start(f32[33,64,64]{2,1,0:T(8,128)} %pad_maximum_fusion.3), channel_id=1, source_target_pairs={{16,0},{32,16},{48,32},{64,48},{80,64},{96,80},{112,96},{128,112},... | collective-permute-start | bytes 1622024 | tf_op jit(solution)/shard_map/ppermute | solution.py:264
  39.0 0.6 reshape.368
  39.6 0.6 iota_add_fusion
  40.3 0.7 fusion.16
  40.9 0.7 slice_bitcast_fusion.1
  41.7 0.9 copy.127.factor_ref
  42.5 0.8 fusion.13
  43.4 0.1 fusion.11
  43.5 0.5 copy-done.14
  44.6 0.1 reduce.8
  44.8 0.1 select_reduce_fusion
  45.1 0.6 gather_fusion
  45.7 0.6 reshape.369.slot_ref
  46.5 0.1 copy.111
  46.8 0.1 copy.113
  47.0 1.0 reshape.352
  48.0 2.2 %pad_maximum_fusion.1 = f32[33,64,64]{2,1,0:T(8,128)} fusion(f32[1,64,64]{2,1,0:T(8,128)S(1)} %pad_bitcast_fusion.4, f32[4,64,64]{2,1,0:T(8,128)} %get-tuple-element.36, f32[16,64,64]{2,1,0:T(8,128)S(1)} %bitcast.60, f32[12,64,64]{2,1,0:T(8,128)} %bitcast.64), kind=kLoop, calls=%fused_computation.4 | loop fusion | flops 405504 | bytes 1081344 | tf_op jit(solution)/shard_map/concatenate | solution.py:249
  50.1 1.1 %pad_maximum_fusion.2 = f32[33,64,64]{2,1,0:T(8,128)} fusion(f32[1,64,64]{2,1,0:T(8,128)S(1)} %pad_bitcast_fusion.3, f32[4,64,64]{2,1,0:T(8,128)S(1)} %copy-done.8, f32[16,64,64]{2,1,0:T(8,128)S(1)} %bitcast.59, f32[12,64,64]{2,1,0:T(8,128)S(1)} %bitcast.63), kind=kLoop, calls=%fused_computation.5 | loop fusion | flops 405504 | bytes 1081344 | tf_op jit(solution)/shard_map/concatenate | solution.py:249
  51.2 1.1 pad_maximum_fusion
  52.3 1.9 %collective-permute-start.1 = (f32[33,64,64]{2,1,0:T(8,128)}, f32[33,64,64]{2,1,0:T(8,128)S(1)}, u32[]{:S(2)}, u32[]{:S(2)}) collective-permute-start(f32[33,64,64]{2,1,0:T(8,128)} %pad_maximum_fusion), channel_id=1, source_target_pairs={{0,16},{16,32},{32,48},{48,64},{64,80},{80,96},{96,112},{112,128},... | collective-permute-start | bytes 1622024 | tf_op jit(solution)/shard_map/ppermute | solution.py:263
  54.3 0.7 slice_convert_fusion.7
  54.9 1.9 %collective-permute-start.4 = (f32[33,64,64]{2,1,0:T(8,128)}, f32[33,64,64]{2,1,0:T(8,128)S(1)}, u32[]{:S(2)}, u32[]{:S(2)}) collective-permute-start(f32[33,64,64]{2,1,0:T(8,128)} %pad_maximum_fusion.2), channel_id=1, source_target_pairs={{1,0},{2,1},{3,2},{4,3},{5,4},{6,5},{7,6},{8,7},{9,8},{10,9},{11,1... | collective-permute-start | bytes 1622024 | tf_op jit(solution)/shard_map/ppermute | solution.py:266
  56.9 0.7 slice_convert_fusion.4
  57.5 4.8 %collective-permute-start.3 = (f32[33,64,64]{2,1,0:T(8,128)}, f32[33,64,64]{2,1,0:T(8,128)S(1)}, u32[]{:S(2)}, u32[]{:S(2)}) collective-permute-start(f32[33,64,64]{2,1,0:T(8,128)} %pad_maximum_fusion.1), channel_id=1, source_target_pairs={{0,1},{1,2},{2,3},{3,4},{4,5},{5,6},{6,7},{7,8},{8,9},{9,10},{10,1... | collective-permute-start | bytes 1622024 | tf_op jit(solution)/shard_map/ppermute | solution.py:265
  62.4 0.7 slice_convert_fusion.2
  63.4 0.7 slice_convert_fusion.9
  64.1 0.7 fusion.5
  64.9 0.1 copy.118
  65.0 15.1 %collective-permute-done.1.xlo_ref = f32[33,64,64]{2,1,0:T(8,128)S(1)} collective-permute-done((f32[33,64,64]{2,1,0:T(8,128)}, f32[33,64,64]{2,1,0:T(8,128)S(1)}, u32[]{:S(2)}, u32[]{:S(2)}) %collective-permute-start.1) | collective-permute-done | bytes 540704 | tf_op jit(solution)/shard_map/ppermute | solution.py:263
  80.3 0.1 copy.108
  80.5 0.1 copy.115
  80.7 0.1 copy.114
  80.9 0.1 copy.120
  81.1 0.7 reshape.365.side_ref
  81.7 0.1 copy-done.5
  81.9 20.4 %shard_map.59 = (f32[32,1,128]{2,1,0:T(1,128)}, bf16[12,14,64,64]{3,2,1,0:T(8,128)(2,1)}) custom-call(s32[128]{0:T(128)} %reshape.365.side_ref, s32[48]{0:T(128)} %reshape.369.slot_ref, f32[4,4,64,64]{3,2,1,0:T(8,128)} %copy-done, f32[4,4,2,64,64]{4,3,2,1,0:T(8,128)} %copy-done.1, f32[4,4,64,64]{3,2,1,0:T(8,128)} %copy.127.factor_ref, ...), custom_call_target="tpu_custom_call" | custom-call | tf_op jit(solution)/shard_map/pallas_call | solution.py:206
  102.3 1.0 slice_reduce_fusion
  103.4 0.7 copy.126
  104.1 5.0 %reshape.370 = bf16[12,14,4096]{2,1,0:T(8,128)(2,1)} reshape(bf16[12,14,64,64]{3,2,1,0:T(8,128)(2,1)} %get-tuple-element.5) | data formatting | bytes 2752512 | tf_op jit(solution)/shard_map/reshape | solution.py:350
  (84 shorter events, 2.7 us)
Async XLA Ops:
  0.6 4.1 %copy-start.7 = (f32[4,4,2,4096]{3,2,1,0:T(2,128)S(1)}, f32[4,4,2,4096]{3,2,1,0:T(2,128)}, u32[]{:S(2)}) copy-start(f32[4,4,2,4096]{3,2,1,0:T(2,128)} %param.5) | copy-start | bytes 1572868
  5.7 1.2 %copy-start.2 = (f32[4,4,2,64,64]{4,3,2,1,0:T(8,128)}, f32[4,4,2,64,64]{4,3,2,1,0:T(8,128)S(1)}, u32[]{:S(2)}) copy-start(f32[4,4,2,64,64]{4,3,2,1,0:T(8,128)S(1)} %reshape.349.minus_ref) | copy-start | bytes 1572868
  6.3 36.3 %copy-start = (f32[4,4,64,64]{3,2,1,0:T(8,128)}, f32[4,4,64,64]{3,2,1,0:T(8,128)S(1)}, u32[]{:S(2)}) copy-start(f32[4,4,64,64]{3,2,1,0:T(8,128)S(1)} %convolution_multiply_fusion.fine_ref) | copy-start | bytes 786436
  6.9 36.5 %copy-start.1 = (f32[4,4,2,64,64]{4,3,2,1,0:T(8,128)}, f32[4,4,2,64,64]{4,3,2,1,0:T(8,128)S(1)}, u32[]{:S(2)}) copy-start(f32[4,4,2,64,64]{4,3,2,1,0:T(8,128)S(1)} %convolution_bitcast_fusion.lead_ref) | copy-start | bytes 1572868
  7.0 20.5 %copy-start.9 = (s32[4,4,2]{1,2,0:T(2,128)S(1)}, s32[4,4,2]{1,2,0:T(2,128)}, u32[]{:S(2)}) copy-start(s32[4,4,2]{1,2,0:T(2,128)} %param.6) | copy-start | bytes 388
  7.0 21.1 %copy-start.6 = (f32[4,4,4096]{2,1,0:T(4,128)S(1)}, f32[4,4,4096]{2,1,0:T(4,128)}, u32[]{:S(2)}) copy-start(f32[4,4,4096]{2,1,0:T(4,128)} %param.4) | copy-start | bytes 786436
  7.7 44.6 %collective-permute-start.2 = (f32[7,64,64]{2,1,0:T(8,128)}, f32[7,64,64]{2,1,0:T(8,128)}, u32[]{:S(2)}, u32[]{:S(2)}) collective-permute-start(f32[7,64,64]{2,1,0:T(8,128)} %pad_maximum_fusion.5), channel_id=1, source_target_pairs={{1,16},{2,17},{3,18},{4,19},{5,20},{6,21},{7,22},{8,23},{9,24},{10... | collective-permute-start | bytes 344072 | tf_op jit(solution)/shard_map/ppermute | solution.py:283
  12.2 42.7 %collective-permute-start.5 = (f32[7,64,64]{2,1,0:T(8,128)}, f32[7,64,64]{2,1,0:T(8,128)}, u32[]{:S(2)}, u32[]{:S(2)}) collective-permute-start(f32[7,64,64]{2,1,0:T(8,128)} %pad_maximum_fusion.6), channel_id=1, source_target_pairs={{16,1},{17,2},{18,3},{19,4},{20,5},{21,6},{22,7},{23,8},{24,9},{25... | collective-permute-start | bytes 344072 | tf_op jit(solution)/shard_map/ppermute | solution.py:283
  19.1 38.4 %collective-permute-start.7 = (f32[7,64,64]{2,1,0:T(8,128)}, f32[7,64,64]{2,1,0:T(8,128)}, u32[]{:S(2)}, u32[]{:S(2)}) collective-permute-start(f32[7,64,64]{2,1,0:T(8,128)} %pad_maximum_fusion.7), channel_id=1, source_target_pairs={{17,0},{18,1},{19,2},{20,3},{21,4},{22,5},{23,6},{24,7},{25,8},{26... | collective-permute-start | bytes 344072 | tf_op jit(solution)/shard_map/ppermute | solution.py:283
  21.8 41.6 %collective-permute-start = (f32[7,64,64]{2,1,0:T(8,128)}, f32[7,64,64]{2,1,0:T(8,128)}, u32[]{:S(2)}, u32[]{:S(2)}) collective-permute-start(f32[7,64,64]{2,1,0:T(8,128)} %pad_maximum_fusion.4), channel_id=1, source_target_pairs={{0,17},{1,18},{2,19},{3,20},{4,21},{5,22},{6,23},{7,24},{8,25},{9,... | collective-permute-start | bytes 344072 | tf_op jit(solution)/shard_map/ppermute | solution.py:283
  32.1 6.9 %copy-start.10 = (s32[4,4]{1,0:T(4,128)S(1)}, s32[4,4]{1,0:T(4,128)}, u32[]{:S(2)}) copy-start(s32[4,4]{1,0:T(4,128)} %param.7) | copy-start | bytes 196
  34.3 29.8 %collective-permute-start.6 = (f32[33,64,64]{2,1,0:T(8,128)}, f32[33,64,64]{2,1,0:T(8,128)}, u32[]{:S(2)}, u32[]{:S(2)}) collective-permute-start(f32[33,64,64]{2,1,0:T(8,128)} %pad_maximum_fusion.3), channel_id=1, source_target_pairs={{16,0},{32,16},{48,32},{64,48},{80,64},{96,80},{112,96},{128,112},... | collective-permute-start | bytes 1622024 | tf_op jit(solution)/shard_map/ppermute | solution.py:264
  43.4 0.6 copy-start.14
  43.4 0.7 copy-start.13
  43.4 0.7 copy-start.15
  43.4 0.9 copy-start.12
  43.4 3.0 %copy-start.11 = (s32[4,2,2]{1,2,0:T(2,128)S(1)}, s32[4,2,2]{1,2,0:T(2,128)}, u32[]{:S(2)}) copy-start(s32[4,2,2]{1,2,0:T(2,128)} %get-tuple-element.46) | copy-start | bytes 196
  48.0 2.2 %copy-start.8 = (f32[4,64,64]{2,1,0:T(8,128)S(1)}, f32[4,64,64]{2,1,0:T(8,128)}, u32[]{:S(2)}) copy-start(f32[4,64,64]{2,1,0:T(8,128)} %get-tuple-element.37) | copy-start | bytes 196612
  52.3 27.8 %collective-permute-start.1 = (f32[33,64,64]{2,1,0:T(8,128)}, f32[33,64,64]{2,1,0:T(8,128)S(1)}, u32[]{:S(2)}, u32[]{:S(2)}) collective-permute-start(f32[33,64,64]{2,1,0:T(8,128)} %pad_maximum_fusion), channel_id=1, source_target_pairs={{0,16},{16,32},{32,48},{48,64},{64,80},{80,96},{96,112},{112,128},... | collective-permute-start | bytes 1622024 | tf_op jit(solution)/shard_map/ppermute | solution.py:263
  54.9 25.4 %collective-permute-start.4 = (f32[33,64,64]{2,1,0:T(8,128)}, f32[33,64,64]{2,1,0:T(8,128)S(1)}, u32[]{:S(2)}, u32[]{:S(2)}) collective-permute-start(f32[33,64,64]{2,1,0:T(8,128)} %pad_maximum_fusion.2), channel_id=1, source_target_pairs={{1,0},{2,1},{3,2},{4,3},{5,4},{6,5},{7,6},{8,7},{9,8},{10,9},{11,1... | collective-permute-start | bytes 1622024 | tf_op jit(solution)/shard_map/ppermute | solution.py:266
  57.5 23.1 %collective-permute-start.3 = (f32[33,64,64]{2,1,0:T(8,128)}, f32[33,64,64]{2,1,0:T(8,128)S(1)}, u32[]{:S(2)}, u32[]{:S(2)}) collective-permute-start(f32[33,64,64]{2,1,0:T(8,128)} %pad_maximum_fusion.1), channel_id=1, source_target_pairs={{0,1},{1,2},{2,3},{3,4},{4,5},{5,6},{6,7},{7,8},{8,9},{9,10},{10,1... | collective-permute-start | bytes 1622024 | tf_op jit(solution)/shard_map/ppermute | solution.py:265
  80.2 1.6 %copy-start.3 = (f32[33,64,64]{2,1,0:T(8,128)}, f32[33,64,64]{2,1,0:T(8,128)S(1)}, u32[]{:S(2)}) copy-start(f32[33,64,64]{2,1,0:T(8,128)S(1)} %collective-permute-done.1.xlo_ref) | copy-start | bytes 1622020
  80.4 1.4 %copy-start.4 = (f32[33,64,64]{2,1,0:T(8,128)}, f32[33,64,64]{2,1,0:T(8,128)S(1)}, u32[]{:S(2)}) copy-start(f32[33,64,64]{2,1,0:T(8,128)S(1)} %collective-permute-done.4.yhi_ref) | copy-start | bytes 1622020
  80.6 1.3 %copy-start.5 = (f32[33,64,64]{2,1,0:T(8,128)}, f32[33,64,64]{2,1,0:T(8,128)S(1)}, u32[]{:S(2)}) copy-start(f32[33,64,64]{2,1,0:T(8,128)S(1)} %collective-permute-done.3.ylo_ref) | copy-start | bytes 1622020

commit v3 on v2

--- a/solution.py
+++ b/solution.py
@@ -147,7 +147,7 @@
         yg[i, j, 1] = dot3(split(wg[i, j, 1]), split(pg[i + 1, j + 2 * sy]))
         return carry
 
-    lax.fori_loop(0, wide_x * wide_y, near_step, 0, unroll=4)
+    lax.fori_loop(0, wide_x * wide_y, near_step, 0, unroll=8)
 
     def far_step(p, carry):
         i = p // (ny + 2)
@@ -163,7 +163,7 @@
             zg[i, j, 3 + 3 * e] = dot3(lead, split(yg[ui, uj, 1]))
         return carry
 
-    lax.fori_loop(0, (nx + 2) * (ny + 2), far_step, 0, unroll=4)
+    lax.fori_loop(0, (nx + 2) * (ny + 2), far_step, 0, unroll=8)
 
     def strong_step(p, carry):
         i = p // ny
@@ -177,7 +177,7 @@
             strong_ref[p * 2 + d] = jnp.broadcast_to(total * (1.0 / scaled.size), (1, 128))
         return carry
 
-    lax.fori_loop(0, nx * ny, strong_step, 0, unroll=4)
+    lax.fori_loop(0, nx * ny, strong_step, 0, unroll=8)
 
     def slot_step(s, carry):
         cell = slot_ref[s * 4]
@@ -194,7 +194,7 @@
                 restrict_ref[s, d * 7 + w] = (row * weight).astype(restrict_ref.dtype)
         return carry
 
-    lax.fori_loop(0, restrict_ref.shape[0], slot_step, 0, unroll=4)
+    lax.fori_loop(0, restrict_ref.shape[0], slot_step, 0, unroll=8)
 
 
 def local_compute(side_flat, slot_table, fine_own, lead_own, factor_own, minus_own, buffers):
@@ -260,10 +260,14 @@
     low = {d: slice(0, d) for d in (1, 2, 3)}
     high_x = {d: slice(nx - d, nx) for d in (1, 2, 3)}
     high_y = {d: slice(ny - d, ny) for d in (1, 2, 3)}
-    from_xlo = lax.ppermute(face(high_x, every), "gx", shift_pairs(n_gx, 1))
-    from_xhi = lax.ppermute(face(low, every), "gx", shift_pairs(n_gx, -1))
-    from_ylo = lax.ppermute(face(every, high_y), "gy", shift_pairs(n_gy, 1))
-    from_yhi = lax.ppermute(face(every, low), "gy", shift_pairs(n_gy, -1))
+    def send_flat(buffer, axis, pairs):
+        arrived = lax.ppermute(buffer.reshape(buffer.shape[0], flat), axis, pairs)
+        return arrived.reshape(buffer.shape)
+
+    from_xlo = send_flat(face(high_x, every), "gx", shift_pairs(n_gx, 1))
+    from_xhi = send_flat(face(low, every), "gx", shift_pairs(n_gx, -1))
+    from_ylo = send_flat(face(every, high_y), "gy", shift_pairs(n_gy, 1))
+    from_yhi = send_flat(face(every, low), "gy", shift_pairs(n_gy, -1))
 
     corners = {}
     for sx in (1, -1):

time: 110 us -> 112 us (1.018)
  local copies, waits for them, and re-layouts: 23 us -> 32.3 us
  waiting for transfers between devices: 15.2 us -> 11.1 us
  other arithmetic: 17.5 us -> 15.4 us
  Pallas kernels: 20.4 us -> 18.7 us
    concatenate x0 -> x15, local copies, waits for them, and re-layouts: none -> 6.6 us  [face(): jnp.concatenate([fine_own[rows[3], cols[3]].reshape((-1,) + blk), lead_ow...]
    ppermute x4, waiting for transfers between devices: 15.2 us -> 11.1 us  [send_flat(): arrived = lax.ppermute(buffer.reshape(buffer.shape[0], flat), axis, pairs)]
    concatenate x4, other arithmetic: 6.53 us -> 3.86 us  [face(): jnp.concatenate([fine_own[rows[3], cols[3]].reshape((-1,) + blk), lead_ow...]
    pallas_call x1, Pallas kernels: 20.4 us -> 18.7 us  [local_compute(): pl.pallas_call(local_kernel, out_shape=(jax.ShapeDtypeStruct((nx * ny * 2...]
    reshape x3 -> x4, local copies, waits for them, and re-layouts: 3.32 us -> 4.95 us  [send_flat(): return arrived.reshape(buffer.shape)]
    convert_element_type x8, local copies, waits for them, and re-layouts: 0.75 us -> 2.05 us  [code_block(): values = codes.reshape(1, -1).astype(jnp.float32)]
    unnamed x40 -> x55, local copies, waits for them, and re-layouts: 3.12 us -> 2.91 us
  transfers between devices with their start and end apart: 8 -> 8, of which waited for: 1 -> 2; matrix products, arithmetic and copies ran while one was open for 24% -> 27% of each run, Pallas kernels for 0% -> 0%
where the time goes in v3:
time: 112 us; the launch traced here: 111 us
  local copies, waits for them, and re-layouts  32.3 us (29%)
  starting transfers between devices  31.1 us (28%)
  Pallas kernels  18.7 us (17%)
  other arithmetic  15.4 us (14%)
  waiting for transfers between devices  11.1 us (10%)
  matrix products  1.16 us (1%)
    pallas_call x1, Pallas kernels, local_compute(): pl.pallas_call(local_kernel, out_shape=(jax.ShapeDtypeStruct((nx * ny * 2...  18.7 us
    ppermute x4, starting transfers between devices, on_device(): lax.ppermute(buffer, ('gx', 'gy'), corner_pairs(n_gx, n_gy, sx, sy))  17.6 us
    ppermute x4, starting transfers between devices, send_flat(): arrived = lax.ppermute(buffer.reshape(buffer.shape[0], flat), axis, pairs)  13.6 us
    ppermute x4, waiting for transfers between devices, send_flat(): arrived = lax.ppermute(buffer.reshape(buffer.shape[0], flat), axis, pairs)  11.1 us
    concatenate x15, local copies, waits for them, and re-layouts, face(): jnp.concatenate([fine_own[rows[3], cols[3]].reshape((-1,) + blk), lead_ow...  6.6 us
    reshape x1, local copies, waits for them, and re-layouts, on_device(): return (strong, restrict.reshape(CAP, 14, flat))  5.02 us
    reshape x4, local copies, waits for them, and re-layouts, send_flat(): return arrived.reshape(buffer.shape)  4.95 us
    concatenate x4, other arithmetic, face(): jnp.concatenate([fine_own[rows[3], cols[3]].reshape((-1,) + blk), lead_ow...  3.86 us
  transfers between devices with their start and end apart: 8, of which 2 were waited for; matrix products, arithmetic and copies ran while one was open for 27% of the time, Pallas kernels for 0%

profile of v3, /device:TPU:103, one launch (start us, length us, event | category | flops | bytes accessed | tf_op | source)
XLA Modules:
  0.0 110.9 jit_solution(5591376673924415361)
XLA Ops:
  0.6 0.7 subtract_convert_fusion
  1.4 1.0 convert_reduce_fusion.4
  2.4 0.8 compare_and_fusion.1
  3.4 0.6 pad_bitcast_fusion.2
  4.0 1.2 %reshape.371.factor_ref = f32[4,4,64,64]{3,2,1,0:T(8,128)S(1)} reshape(f32[4,4,4096]{2,1,0:T(4,128)} %param.4) | data formatting | bytes 524288 | tf_op jit(solution)/shard_map/reshape | solution.py:242
  5.2 0.3 broadcast_multiply_fusion
  5.5 0.6 reshape.373.minus_ref
  6.1 0.6 convolution_multiply_fusion.fine_ref
  6.8 0.3 copy-done.3
  7.1 0.6 convolution_bitcast_fusion.lead_ref
  7.9 0.9 pad_maximum_fusion.5
  8.7 3.8 %collective-permute-start.2 = (f32[7,64,64]{2,1,0:T(8,128)}, f32[7,64,64]{2,1,0:T(8,128)}, u32[]{:S(2)}, u32[]{:S(2)}) collective-permute-start(f32[7,64,64]{2,1,0:T(8,128)} %pad_maximum_fusion.5), channel_id=1, source_target_pairs={{1,16},{2,17},{3,18},{4,19},{5,20},{6,21},{7,22},{8,23},{9,24},{10... | collective-permute-start | bytes 344072 | tf_op jit(solution)/shard_map/ppermute | solution.py:287
  12.5 0.7 pad_maximum_fusion.6
  13.2 6.2 %collective-permute-start.5 = (f32[7,64,64]{2,1,0:T(8,128)}, f32[7,64,64]{2,1,0:T(8,128)}, u32[]{:S(2)}, u32[]{:S(2)}) collective-permute-start(f32[7,64,64]{2,1,0:T(8,128)} %pad_maximum_fusion.6), channel_id=1, source_target_pairs={{16,1},{17,2},{18,3},{19,4},{20,5},{21,6},{22,7},{23,8},{24,9},{25... | collective-permute-start | bytes 344072 | tf_op jit(solution)/shard_map/ppermute | solution.py:287
  19.4 0.7 pad_maximum_fusion.7
  20.1 1.9 %collective-permute-start.7 = (f32[7,64,64]{2,1,0:T(8,128)}, f32[7,64,64]{2,1,0:T(8,128)}, u32[]{:S(2)}, u32[]{:S(2)}) collective-permute-start(f32[7,64,64]{2,1,0:T(8,128)} %pad_maximum_fusion.7), channel_id=1, source_target_pairs={{17,0},{18,1},{19,2},{20,3},{21,4},{22,5},{23,6},{24,7},{25,8},{26... | collective-permute-start | bytes 344072 | tf_op jit(solution)/shard_map/ppermute | solution.py:287
  22.1 0.7 pad_maximum_fusion.4
  22.8 5.7 %collective-permute-start = (f32[7,64,64]{2,1,0:T(8,128)}, f32[7,64,64]{2,1,0:T(8,128)}, u32[]{:S(2)}, u32[]{:S(2)}) collective-permute-start(f32[7,64,64]{2,1,0:T(8,128)} %pad_maximum_fusion.4), channel_id=1, source_target_pairs={{0,17},{1,18},{2,19},{3,20},{4,21},{5,22},{6,23},{7,24},{8,25},{9,... | collective-permute-start | bytes 344072 | tf_op jit(solution)/shard_map/ppermute | solution.py:287
  28.5 0.7 fusion.15
  29.2 0.7 fusion.13
  30.4 0.6 pad.48
  31.0 1.4 %concatenate.96 = f32[1,4096]{1,0:T(1,128)} reshape(f32[64,64]{1,0:T(8,128)} %pad.48) | data formatting | bytes 32768 | tf_op jit(solution)/shard_map/concatenate | solution.py:249
  32.5 0.7 concatenate.95
  33.2 0.9 concatenate.93
  34.2 1.9 %pad_maximum_fusion.2 = f32[33,4096]{1,0:T(8,128)} fusion(f32[1,4096]{1,0:T(1,128)} %concatenate.96, f32[4,4096]{1,0:T(4,128)} %concatenate.95, f32[16,4096]{1,0:T(8,128)S(1)} %concatenate.94, f32[12,4096]{1,0:T(8,128)} %concatenate.93), kind=kLoop, calls=%fused_computation.5 | loop fusion | flops 405504 | bytes 1081344 | tf_op jit(solution)/shard_map/concatenate | solution.py:249
  36.2 1.9 %collective-permute-start.4 = (f32[33,4096]{1,0:T(8,128)}, f32[33,4096]{1,0:T(8,128)}, u32[]{:S(2)}, u32[]{:S(2)}) collective-permute-start(f32[33,4096]{1,0:T(8,128)} %pad_maximum_fusion.2), channel_id=1, source_target_pairs={{1,0},{2,1},{3,2},{4,3},{5,4},{6,5},{7,6},{8,7},{9,8},{10,9},{11,1... | collective-permute-start | bytes 1622024 | tf_op jit(solution)/shard_map/ppermute | solution.py:264
  38.1 0.6 reshape.384
  38.7 0.5 iota_add_fusion
  39.3 0.6 slice_convert_fusion.1
  39.9 0.7 slice_bitcast_fusion.5
  40.6 0.8 fusion.11
  41.6 0.5 copy-done.22
  42.4 0.7 copy.92
  43.2 0.8 copy.102
  44.2 0.6 sub.25
  44.8 0.7 select_reduce_fusion
  46.1 0.7 concatenate.90
  46.8 0.9 concatenate.88
  48.0 0.2 concatenate.89
  48.4 0.2 concatenate.101
  48.6 0.4 copy-done.9
  49.0 0.2 copy-done.15
  49.2 0.9 pad_maximum_fusion
  50.2 0.9 pad_maximum_fusion.3
  51.4 0.6 gather_fusion
  52.0 0.6 reshape.385.slot_ref
  52.6 4.8 %collective-permute-start.3 = (f32[33,4096]{1,0:T(8,128)S(1)}, f32[33,4096]{1,0:T(8,128)S(1)}, u32[]{:S(2)}, u32[]{:S(2)}) collective-permute-start(f32[33,4096]{1,0:T(8,128)S(1)} %pad_maximum_fusion.1), channel_id=1, source_target_pairs={{0,1},{1,2},{2,3},{3,4},{4,5},{5,6},{6,7},{7,8},{8,9},{9,10},{10,1... | collective-permute-start | bytes 1622024 | tf_op jit(solution)/shard_map/ppermute | solution.py:264
  57.5 0.7 slice_convert_fusion.7
  58.2 4.7 %collective-permute-start.6 = (f32[33,4096]{1,0:T(8,128)}, f32[33,4096]{1,0:T(8,128)}, u32[]{:S(2)}, u32[]{:S(2)}) collective-permute-start(f32[33,4096]{1,0:T(8,128)} %pad_maximum_fusion.3), channel_id=1, source_target_pairs={{16,0},{32,16},{48,32},{64,48},{80,64},{96,80},{112,96},{128,112},... | collective-permute-start | bytes 1622024 | tf_op jit(solution)/shard_map/ppermute | solution.py:264
  62.9 0.7 slice_convert_fusion.4
  63.6 2.1 %collective-permute-start.1 = (f32[33,4096]{1,0:T(8,128)}, f32[33,4096]{1,0:T(8,128)}, u32[]{:S(2)}, u32[]{:S(2)}) collective-permute-start(f32[33,4096]{1,0:T(8,128)} %pad_maximum_fusion), channel_id=1, source_target_pairs={{0,16},{16,32},{32,48},{48,64},{64,80},{80,96},{96,112},{112,128},... | collective-permute-start | bytes 1622024 | tf_op jit(solution)/shard_map/ppermute | solution.py:264
  65.7 0.7 slice_convert_fusion.2
  66.7 0.7 slice_convert_fusion.9
  67.4 1.5 %reshape.377.yhi_ref = f32[33,64,64]{2,1,0:T(8,128)S(1)} reshape(f32[33,4096]{1,0:T(8,128)} %collective-permute-done.4) | data formatting | bytes 1081344 | tf_op jit(solution)/shard_map/reshape | solution.py:265
  69.2 0.4 reshape.376.ylo_ref
  69.9 5.9 %collective-permute-done.6 = f32[33,4096]{1,0:T(8,128)} collective-permute-done((f32[33,4096]{1,0:T(8,128)}, f32[33,4096]{1,0:T(8,128)}, u32[]{:S(2)}, u32[]{:S(2)}) %collective-permute-start.6) | collective-permute-done | bytes 540704 | tf_op jit(solution)/shard_map/ppermute | solution.py:264
  75.8 1.5 %reshape.379.xhi_ref = f32[33,64,64]{2,1,0:T(8,128)S(1)} reshape(f32[33,4096]{1,0:T(8,128)} %collective-permute-done.6) | data formatting | bytes 1081344 | tf_op jit(solution)/shard_map/reshape | solution.py:265
  77.5 5.1 %collective-permute-done.1 = f32[33,4096]{1,0:T(8,128)} collective-permute-done((f32[33,4096]{1,0:T(8,128)}, f32[33,4096]{1,0:T(8,128)}, u32[]{:S(2)}, u32[]{:S(2)}) %collective-permute-start.1) | collective-permute-done | bytes 540704 | tf_op jit(solution)/shard_map/ppermute | solution.py:264
  82.7 1.5 %reshape.374.xlo_ref = f32[33,64,64]{2,1,0:T(8,128)S(1)} reshape(f32[33,4096]{1,0:T(8,128)} %collective-permute-done.1) | data formatting | bytes 1081344 | tf_op jit(solution)/shard_map/reshape | solution.py:265
  84.6 0.7 reshape.381.side_ref
  85.3 18.7 %shard_map.59 = (f32[32,1,128]{2,1,0:T(1,128)}, bf16[12,14,64,64]{3,2,1,0:T(8,128)(2,1)}) custom-call(s32[128]{0:T(128)} %reshape.381.side_ref, s32[48]{0:T(128)} %reshape.385.slot_ref, f32[4,4,64,64]{3,2,1,0:T(8,128)} %copy-done, f32[4,4,2,64,64]{4,3,2,1,0:T(8,128)} %copy-done.1, f32[4,4,64,64]{3,2,1,0:T(8,128)} %copy-done.2, ...), custom_call_target="tpu_custom_call" | custom-call | tf_op jit(solution)/shard_map/pallas_call | solution.py:206
  104.0 1.0 slice_reduce_fusion
  105.2 0.7 copy.111
  105.9 5.0 %reshape.386 = bf16[12,14,4096]{2,1,0:T(8,128)(2,1)} reshape(bf16[12,14,64,64]{3,2,1,0:T(8,128)(2,1)} %get-tuple-element.5) | data formatting | bytes 2752512 | tf_op jit(solution)/shard_map/reshape | solution.py:354
  (114 shorter events, 4.9 us)
Async XLA Ops:
  0.6 4.6 %copy-start.11 = (f32[4,4,2,4096]{3,2,1,0:T(2,128)S(1)}, f32[4,4,2,4096]{3,2,1,0:T(2,128)}, u32[]{:S(2)}) copy-start(f32[4,4,2,4096]{3,2,1,0:T(2,128)} %param.5) | copy-start | bytes 1572868
  5.2 24.0 %copy-start.2 = (f32[4,4,64,64]{3,2,1,0:T(8,128)}, f32[4,4,64,64]{3,2,1,0:T(8,128)S(1)}, u32[]{:S(2)}) copy-start(f32[4,4,64,64]{3,2,1,0:T(8,128)S(1)} %reshape.371.factor_ref) | copy-start | bytes 786436
  6.1 1.0 copy-start.3
  6.7 33.9 %copy-start = (f32[4,4,64,64]{3,2,1,0:T(8,128)}, f32[4,4,64,64]{3,2,1,0:T(8,128)S(1)}, u32[]{:S(2)}) copy-start(f32[4,4,64,64]{3,2,1,0:T(8,128)S(1)} %convolution_multiply_fusion.fine_ref) | copy-start | bytes 786436
  7.1 0.8 copy-start.17
  7.7 33.8 %copy-start.1 = (f32[4,4,2,64,64]{4,3,2,1,0:T(8,128)}, f32[4,4,2,64,64]{4,3,2,1,0:T(8,128)S(1)}, u32[]{:S(2)}) copy-start(f32[4,4,2,64,64]{4,3,2,1,0:T(8,128)S(1)} %convolution_bitcast_fusion.lead_ref) | copy-start | bytes 1572868
  7.7 20.8 %copy-start.16 = (s32[4,4,2]{1,2,0:T(2,128)S(1)}, s32[4,4,2]{1,2,0:T(2,128)}, u32[]{:S(2)}) copy-start(s32[4,4,2]{1,2,0:T(2,128)} %param.6) | copy-start | bytes 388
  8.7 43.9 %collective-permute-start.2 = (f32[7,64,64]{2,1,0:T(8,128)}, f32[7,64,64]{2,1,0:T(8,128)}, u32[]{:S(2)}, u32[]{:S(2)}) collective-permute-start(f32[7,64,64]{2,1,0:T(8,128)} %pad_maximum_fusion.5), channel_id=1, source_target_pairs={{1,16},{2,17},{3,18},{4,19},{5,20},{6,21},{7,22},{8,23},{9,24},{10... | collective-permute-start | bytes 344072 | tf_op jit(solution)/shard_map/ppermute | solution.py:287
  13.2 44.9 %collective-permute-start.5 = (f32[7,64,64]{2,1,0:T(8,128)}, f32[7,64,64]{2,1,0:T(8,128)}, u32[]{:S(2)}, u32[]{:S(2)}) collective-permute-start(f32[7,64,64]{2,1,0:T(8,128)} %pad_maximum_fusion.6), channel_id=1, source_target_pairs={{16,1},{17,2},{18,3},{19,4},{20,5},{21,6},{22,7},{23,8},{24,9},{25... | collective-permute-start | bytes 344072 | tf_op jit(solution)/shard_map/ppermute | solution.py:287
  20.1 43.5 %collective-permute-start.7 = (f32[7,64,64]{2,1,0:T(8,128)}, f32[7,64,64]{2,1,0:T(8,128)}, u32[]{:S(2)}, u32[]{:S(2)}) collective-permute-start(f32[7,64,64]{2,1,0:T(8,128)} %pad_maximum_fusion.7), channel_id=1, source_target_pairs={{17,0},{18,1},{19,2},{20,3},{21,4},{22,5},{23,6},{24,7},{25,8},{26... | collective-permute-start | bytes 344072 | tf_op jit(solution)/shard_map/ppermute | solution.py:287
  22.8 43.9 %collective-permute-start = (f32[7,64,64]{2,1,0:T(8,128)}, f32[7,64,64]{2,1,0:T(8,128)}, u32[]{:S(2)}, u32[]{:S(2)}) collective-permute-start(f32[7,64,64]{2,1,0:T(8,128)} %pad_maximum_fusion.4), channel_id=1, source_target_pairs={{0,17},{1,18},{2,19},{3,20},{4,21},{5,22},{6,23},{7,24},{8,25},{9,... | collective-permute-start | bytes 344072 | tf_op jit(solution)/shard_map/ppermute | solution.py:287
  34.1 4.0 %copy-start.18 = (s32[4,4]{1,0:T(4,128)S(1)}, s32[4,4]{1,0:T(4,128)}, u32[]{:S(2)}) copy-start(s32[4,4]{1,0:T(4,128)} %param.7) | copy-start | bytes 196
  34.1 5.9 %copy-start.10 = (f32[4,4,4096]{2,1,0:T(4,128)S(1)}, f32[4,4,4096]{2,1,0:T(4,128)}, u32[]{:S(2)}) copy-start(f32[4,4,4096]{2,1,0:T(4,128)} %param.4) | copy-start | bytes 786436
  36.2 31.3 %collective-permute-start.4 = (f32[33,4096]{1,0:T(8,128)}, f32[33,4096]{1,0:T(8,128)}, u32[]{:S(2)}, u32[]{:S(2)}) collective-permute-start(f32[33,4096]{1,0:T(8,128)} %pad_maximum_fusion.2), channel_id=1, source_target_pairs={{1,0},{2,1},{3,2},{4,3},{5,4},{6,5},{7,6},{8,7},{9,8},{10,9},{11,1... | collective-permute-start | bytes 1622024 | tf_op jit(solution)/shard_map/ppermute | solution.py:264
  41.5 0.6 copy-start.22
  41.5 0.6 copy-start.20
  41.5 0.6 copy-start.23
  41.5 4.0 %copy-start.19 = (s32[4,2,2]{1,2,0:T(2,128)S(1)}, s32[4,2,2]{1,2,0:T(2,128)}, u32[]{:S(2)}) copy-start(s32[4,2,2]{1,2,0:T(2,128)} %get-tuple-element.46) | copy-start | bytes 196
  41.5 4.6 %copy-start.12 = (f32[4,1,64,64]{3,2,1,0:T(8,128)S(1)}, f32[4,1,64,64]{3,2,1,0:T(8,128)}, u32[]{:S(2)}) copy-start(f32[4,1,64,64]{3,2,1,0:T(8,128)} %get-tuple-element.36) | copy-start | bytes 196612
  42.1 5.6 %copy-start.8 = (f32[3,4,64,64]{3,2,1,0:T(8,128)S(1)}, f32[3,4,64,64]{3,2,1,0:T(8,128)}, u32[]{:S(2)}) copy-start(f32[3,4,64,64]{3,2,1,0:T(8,128)} %get-tuple-element.32) | copy-start | bytes 589828
  48.0 1.0 copy-start.9
  48.0 0.9 copy-start.13
  48.4 0.9 copy-start.15
  48.9 1.2 %copy-start.14 = (f32[4,4096]{1,0:T(4,128)S(1)}, f32[4,4096]{1,0:T(4,128)}, u32[]{:S(2)}) copy-start(f32[4,4096]{1,0:T(4,128)} %get-tuple-element.43) | copy-start | bytes 196612
  49.2 1.9 %copy-start.21 = (s32[12]{0:T(128)S(1)}, s32[12]{0:T(128)}, u32[]{:S(2)}) copy-start(s32[12]{0:T(128)} %get-tuple-element.23) | copy-start | bytes 148
  52.6 16.5 %collective-permute-start.3 = (f32[33,4096]{1,0:T(8,128)S(1)}, f32[33,4096]{1,0:T(8,128)S(1)}, u32[]{:S(2)}, u32[]{:S(2)}) collective-permute-start(f32[33,4096]{1,0:T(8,128)S(1)} %pad_maximum_fusion.1), channel_id=1, source_target_pairs={{0,1},{1,2},{2,3},{3,4},{4,5},{5,6},{6,7},{7,8},{8,9},{9,10},{10,1... | collective-permute-start | bytes 1622024 | tf_op jit(solution)/shard_map/ppermute | solution.py:264
  58.2 17.6 %collective-permute-start.6 = (f32[33,4096]{1,0:T(8,128)}, f32[33,4096]{1,0:T(8,128)}, u32[]{:S(2)}, u32[]{:S(2)}) collective-permute-start(f32[33,4096]{1,0:T(8,128)} %pad_maximum_fusion.3), channel_id=1, source_target_pairs={{16,0},{32,16},{48,32},{64,48},{80,64},{96,80},{112,96},{128,112},... | collective-permute-start | bytes 1622024 | tf_op jit(solution)/shard_map/ppermute | solution.py:264
  63.6 19.1 %collective-permute-start.1 = (f32[33,4096]{1,0:T(8,128)}, f32[33,4096]{1,0:T(8,128)}, u32[]{:S(2)}, u32[]{:S(2)}) collective-permute-start(f32[33,4096]{1,0:T(8,128)} %pad_maximum_fusion), channel_id=1, source_target_pairs={{0,16},{16,32},{32,48},{48,64},{64,80},{80,96},{96,112},{112,128},... | collective-permute-start | bytes 1622024 | tf_op jit(solution)/shard_map/ppermute | solution.py:264
  69.0 8.3 %copy-start.4 = (f32[33,64,64]{2,1,0:T(8,128)}, f32[33,64,64]{2,1,0:T(8,128)S(1)}, u32[]{:S(2)}) copy-start(f32[33,64,64]{2,1,0:T(8,128)S(1)} %reshape.377.yhi_ref) | copy-start | bytes 1622020
  69.6 14.6 %copy-start.5 = (f32[33,64,64]{2,1,0:T(8,128)}, f32[33,64,64]{2,1,0:T(8,128)S(1)}, u32[]{:S(2)}) copy-start(f32[33,64,64]{2,1,0:T(8,128)S(1)} %reshape.376.ylo_ref) | copy-start | bytes 1622020
  77.3 8.0 %copy-start.6 = (f32[33,64,64]{2,1,0:T(8,128)}, f32[33,64,64]{2,1,0:T(8,128)S(1)}, u32[]{:S(2)}) copy-start(f32[33,64,64]{2,1,0:T(8,128)S(1)} %reshape.379.xhi_ref) | copy-start | bytes 1622020
  84.2 1.1 copy-start.7
